TPU v7x, 128 devices: a whole 4x4x4 slice. The times are simulated.
128 devices in a mesh: req: 64 (over z, y, x), col: 2 (over core).
Axes of the slice: x: 4, y: 4, z: 4, core: 2. Of those that a mesh axis runs over, the one named last changes fastest.
Arguments:
- tokens: bfloat16 [32768, 1024], P(('req', 'col')), may hold values from -6 to 6
- norm_gain_pair: float32 [2, 1024], replicated, may hold values from 0.5 to 1.5
- query_key_value_weight: bfloat16 [3, 1024, 1024], P(None, None, 'col'), may hold values from -1 to 1
- head_gate_weight: bfloat16 [2, 1024, 8], P(None, None, 'col'), may hold values from -0.1875 to 0.1875
- decay_logit_bias: float32 [8], P('col'), may hold values from -1 to 1024, as said below
- adapter_down_factor: bfloat16 [64, 1024, 16], P('col'), may hold values from -0.1875 to 0.1875
- adapter_up_factor: bfloat16 [64, 16, 1024], P(None, None, 'col'), may hold values from -1.5 to 1.5
- lengths: int32 [64, 2, 3], P('req'), may hold values from 1 to 128, 256 in all within a row
- request_adapter_index: int32 [64, 6], P('req'), may hold values from 0 to 63
- request_cache_index: int32 [64, 6], P('req'), may hold values from 0 to 511
- caches: bfloat16 [256, 8, 128, 128], P('req', 'col'), may hold values from -6 to 6
- head_output_weight: bfloat16 [1024, 1024], P('col'), may hold values from -0.1875 to 0.1875
- feedforward_weight: bfloat16 [3, 1024, 2816], P(None, None, 'col'), may hold values from -0.1875 to 0.1875
Outputs:
- layer_out: bfloat16 [32768, 1024], P(('req', 'col'))
Inputs may be any that keep to these rules, and one draw needn't show every extreme that they name: The 3 lengths of one device sum to 256, and the longest of them is exactly 128. `request_cache_index`: a value of 256 or more means that the request has no cached memory state. `decay_logit_bias`: at most the logarithm of 512.
All inputs are finite; a program needn't handle non-finite values.
Results may differ from a plain program's by a relative error of at most 0.015.
Values may be sent and summed in bfloat16 or wider, within the bound.
No kernel may reach another device: no remote copies, remote signals or barrier semaphores. Data moves between devices by JAX's collectives and lax.ppermute only.
A program may use at most 192 MiB of HBM per device.

v0:
```python
import math

import jax
import jax.numpy as jnp
from jax import lax
from jax.sharding import PartitionSpec as P

epsilon = 1e-05


def rms_scale(values, gain):
    widened = values.astype(jnp.float32)
    factor = lax.rsqrt(jnp.mean(widened * widened, axis=-1, keepdims=True) + epsilon)
    return (widened * factor * gain).astype(jnp.bfloat16)


def on_device(
    tokens,
    norm_gain_pair,
    query_key_value_weight,
    head_gate_weight,
    decay_logit_bias,
    adapter_down_factor,
    adapter_up_factor,
    lengths,
    request_adapter_index,
    request_cache_index,
    caches,
    head_output_weight,
    feedforward_weight,
):
    tok_rows, width = tokens.shape
    col_count = lax.axis_size("col")
    group = tok_rows * col_count
    head_cols = query_key_value_weight.shape[2]
    local_heads = head_gate_weight.shape[2]
    head_size = head_cols // local_heads
    group_lengths = lengths[0].reshape(-1)
    scale = 1.0 / math.sqrt(head_size)
    normalized_rows = rms_scale(tokens, norm_gain_pair[0])
    gathered = lax.all_gather(normalized_rows, "col", axis=0, tiled=True)
    positions = jnp.arange(group, dtype=jnp.int32)
    ends = jnp.cumsum(group_lengths)
    starts = ends - group_lengths
    member = (
        (positions[:, None] >= starts[None, :]) & (positions[:, None] < ends[None, :])
    ).astype(jnp.float32)
    segment = jnp.sum((positions[:, None] >= ends[None, :]).astype(jnp.int32), axis=1)
    projected = jnp.einsum(
        "td,kdc->ktc", gathered, query_key_value_weight, preferred_element_type=jnp.float32
    )
    token_segment = lax.all_gather(adapter_down_factor, "col", axis=0, tiled=True)
    numbers = jnp.arange(token_segment.shape[0], dtype=jnp.int32)
    select = (request_adapter_index[0][:, None] == numbers[None, :]).astype(jnp.bfloat16)
    chosen = jnp.einsum(
        "sa,adr->sdr", select, token_segment, preferred_element_type=jnp.float32
    ).astype(jnp.bfloat16)
    per_request = jnp.einsum("td,sdr->tsr", gathered, chosen, preferred_element_type=jnp.float32)
    low_rank_delta = jnp.sum(member[:, :, None] * per_request, axis=1)
    low_rank_delta = low_rank_delta.astype(jnp.bfloat16)
    adapter_onehot = (
        request_adapter_index[0][:, None]
        == jnp.arange(adapter_up_factor.shape[0], dtype=jnp.int32)[None, :]
    ).astype(jnp.bfloat16)
    up_chosen = jnp.einsum(
        "gq,qjl->gjl", adapter_onehot, adapter_up_factor, preferred_element_type=jnp.float32
    ).astype(jnp.bfloat16)
    delta_all = jnp.einsum(
        "tr,src->tsc", low_rank_delta, up_chosen, preferred_element_type=jnp.float32
    )
    delta = jnp.sum(member[:, :, None] * delta_all, axis=1)
    queries = (projected[0] + delta).astype(jnp.bfloat16).reshape(group, local_heads, head_size)
    keys = projected[1].astype(jnp.bfloat16).reshape(group, local_heads, head_size)
    values = projected[2].astype(jnp.bfloat16).reshape(group, local_heads, head_size)
    gate_terms = jnp.einsum(
        "td,kdh->kth", gathered, head_gate_weight, preferred_element_type=jnp.float32
    )
    log_keep = jax.nn.log_sigmoid(gate_terms[0] + decay_logit_bias[None, :])
    mix_gate = jax.nn.sigmoid(gate_terms[1])
    running = jnp.cumsum(log_keep, axis=0)
    before = running - log_keep
    start_hot = (positions[None, :] == starts[:, None]).astype(jnp.float32)
    start_level = jnp.sum(start_hot[:, :, None] * before[None, :, :], axis=1)
    level = running - jnp.sum(member[:, :, None] * start_level[None, :, :], axis=1)
    token_segment = lax.all_gather(caches, "req", axis=0, tiled=True)
    numbers = jnp.arange(token_segment.shape[0], dtype=jnp.int32)
    select = (request_cache_index[0][:, None] == numbers[None, :]).astype(jnp.bfloat16)
    states = jnp.einsum(
        "sn,nhij->shij", select, token_segment, preferred_element_type=jnp.float32
    ).astype(jnp.bfloat16)
    from_state = jnp.einsum("thi,shij->tshj", queries, states, preferred_element_type=jnp.float32)
    carried = jnp.sum(member[:, :, None, None] * from_state, axis=1) * jnp.exp(level)[:, :, None]
    block = min(512, group)

    def one_block(index):
        begin = index * block
        scores = (
            jnp.einsum("qhd,khd->hqk", queries, keys, preferred_element_type=jnp.float32) * scale
        )
        q_pos = begin + jnp.arange(block, dtype=jnp.int32)
        allowed = (segment[:, None] == segment[None, :]) & (positions[None, :] <= q_pos[:, None])
        masked = jnp.where(allowed[None], scores, -jnp.inf)
        peak = jnp.max(masked, axis=2, keepdims=True)
        weights = jnp.exp(masked - peak)
        probs = (weights / jnp.sum(weights, axis=2, keepdims=True)).astype(jnp.bfloat16)
        attended = jnp.einsum("hqk,khd->qhd", probs, values, preferred_element_type=jnp.float32)
        gap = jnp.where(allowed[None], running.T[:, :, None] - running.T[:, None, :], -jnp.inf)
        memory_w = (scores * jnp.exp(gap)).astype(jnp.bfloat16)
        recalled = jnp.einsum("hqk,khd->qhd", memory_w, values, preferred_element_type=jnp.float32)
        recalled = recalled + carried
        factor = lax.rsqrt(jnp.mean(recalled * recalled, axis=2, keepdims=True) + epsilon)
        combined = attended + mix_gate[:, :, None] * recalled * factor
        return combined.astype(jnp.bfloat16).reshape(block, head_cols)

    blocks = lax.map(one_block, jnp.arange(group // block, dtype=jnp.int32))
    head_out = blocks.reshape(group, head_cols)
    attn_proj = lax.psum_scatter(
        jnp.dot(head_out, head_output_weight, preferred_element_type=jnp.float32),
        "col",
        scatter_dimension=0,
        tiled=True,
    )
    mixed = (tokens.astype(jnp.float32) + attn_proj).astype(jnp.bfloat16)
    normed_two = rms_scale(mixed, norm_gain_pair[1])
    token_segment = lax.all_gather(feedforward_weight, "col", axis=2, tiled=True)
    gate_up = jnp.einsum(
        "td,kdf->ktf", normed_two, token_segment[:2], preferred_element_type=jnp.float32
    )
    hidden = (jax.nn.silu(gate_up[0]) * gate_up[1]).astype(jnp.bfloat16)
    feed = jnp.einsum("tf,df->td", hidden, token_segment[2], preferred_element_type=jnp.float32)
    return (mixed.astype(jnp.float32) + feed).astype(jnp.bfloat16)


def solution(mesh):
    placed = (
        P(("req", "col"), None),
        P(),
        P(None, None, "col"),
        P(None, None, "col"),
        P("col"),
        P("col", None, None),
        P(None, None, "col"),
        P("req", None, None),
        P("req", None),
        P("req", None),
        P("req", "col", None, None),
        P("col", None),
        P(None, None, "col"),
    )
    return jax.shard_map(
        on_device, mesh=mesh, in_specs=placed, out_specs=P(("req", "col"), None), check_vma=False
    )
```

profile of v0, /device:TPU:1, one launch (start us, length us, event | category | flops | bytes accessed | tf_op | source)
XLA Modules:
  0.0 319.6 jit_solution(7090761878730281534)
XLA Ops:
  6.5 0.0 copy-start
  6.5 1.4 fusion.38
  7.9 1.4 fusion.87
  9.3 2.0 fusion.40
  11.3 0.0 all-gather.5.cloned.1.call-update
  11.3 0.0 all-gather.7.cloned.1.call-start
  11.4 0.7 all-gather.7.cloned.1.call-update
  12.1 0.0 all-gather.9.cloned.1.call-start
  12.1 0.7 all-gather.9.cloned.1.call-update
  12.8 0.0 reduce-scatter.2.cloned.1.call-start
  12.9 0.8 reshape_squeeze.3
  13.6 0.8 reshape.275
  14.4 0.2 reduce-window.14
  14.6 0.1 convert_reduce_fusion
  14.7 0.7 fusion.62
  15.3 0.1 fusion.61
  15.4 0.2 fusion.48
  15.6 2.4 convolution_convert_fusion
  18.1 8.8 %all-gather.5.cloned.1.call-done = bf16[512,1024]{1,0:T(8,128)(2,1)} async-done(((bf16[256,1024]{1,0:T(8,128)(2,1)}), bf16[512,1024]{1,0:T(8,128)(2,1)}) %all-gather.5.cloned.1.call-update) | async-done | bytes 1048592 | tf_op jit(solution)/shard_map/all_gather | solution.py:41
  26.9 1.6 convolution_bitcast_fusion.1
  28.5 0.6 copy-done.8
  29.1 1.3 fusion.84
  30.4 1.3 reshape.277
  31.7 3.0 reduce-window.18
  34.8 1.4 slice_reduce_fusion
  36.2 1.3 reduce-window.19
  37.5 0.8 add_bitcast_fusion
  38.3 0.6 copy.88
  38.9 3.2 %fusion.88 = (bf16[3,512,512]{1,2,0:T(8,128)(2,1)S(1)}, f32[3,512,512]{1,2,0:T(8,128)S(1)}) fusion(bf16[3,1024,512]{2,1,0:T(8,128)(2,1)S(1)} %copy-done, bf16[512,1024]{1,0:T(8,128)(2,1)} %all-gather.5.cloned.1.call-done), kind=kOutput, calls=%fused_computation.113 | convolution fusion | flops 1611399168 | bytes 8912896 | tf_op jit(solution)/shard_map/td,kdc->ktc/dot_general | solution.py:49
  42.1 0.0 copy-start.15
  42.1 0.1 slice.55
  42.2 0.1 bitcast_subtract_fusion.1
  42.3 0.0 copy-done.10
  42.3 0.1 multiply_reduce_fusion.4
  42.4 0.1 multiply_reduce_fusion.3
  42.5 0.6 fusion.69
  43.1 0.6 fusion.70
  43.7 1.0 fusion.86
  44.8 3.9 %fusion.35 = bf16[6,1024,16]{1,0,2:T(8,128)(2,1)S(1)} fusion(bf16[64,1024,16]{1,2,0:T(8,128)(2,1)} %all-gather.7.cloned.1.call-done, s32[6]{0:T(128)S(1)} %bitcast.135), kind=kOutput, calls=%fused_computation.41 | convolution fusion | flops 12681600 | bytes 2293784 | tf_op jit(solution)/shard_map/sa,adr->sdr/dot_general | solution.py:55
  48.7 0.1 copy.48
  48.8 0.5 fusion.92
  49.3 1.0 multiply_reduce_fusion
  50.3 0.3 copy.51
  50.7 0.3 add_convert_fusion
  50.9 0.0 copy-start.17
  50.9 4.8 %fusion.89 = (f32[4,512]{1,0:T(4,128)S(1)}, f32[4,512,512]{1,2,0:T(8,128)}) fusion(pred[512,512]{0,1:T(8,128)(4,1)S(1)} %fusion.48, bf16[512,4,128]{0,2,1:T(8,128)(2,1)S(1)} %add_convert_fusion, bf16[512,4,128]{0,2,1:T(8,128)(2,1)} %bitcast.128), kind=kOutput, calls=%fused_computation.114 | convolution fusion | flops 272630272 | bytes 5513216 | tf_op jit(solution)/shard_map/while/body/eval_jaxpr/sub | solution.py:104
  55.7 152.0 %all-gather.9.cloned.1.call-done = bf16[256,4,128,128]{3,2,1,0:T(8,128)(2,1)} async-done(((bf16[4,4,128,128]{3,2,1,0:T(8,128)(2,1)}), bf16[256,4,128,128]{3,2,1,0:T(8,128)(2,1)}) %all-gather.9.cloned.1.call-update) | async-done | bytes 33554448 | tf_op jit(solution)/shard_map/all_gather | solution.py:85
  207.7 32.0 %fusion.20 = bf16[6,4,128,128]{3,0,2,1:T(8,128)(2,1)S(1)} fusion(bf16[256,4,128,128]{3,2,1,0:T(8,128)(2,1)} %all-gather.9.cloned.1.call-done, s32[6]{0:T(128)S(1)} %bitcast.138), kind=kOutput, calls=%fused_computation.33 | convolution fusion | flops 201721344 | bytes 34340888 | tf_op jit(solution)/shard_map/sn,nhij->shij/dot_general | solution.py:88
  239.8 0.0 copy-start.6
  239.8 2.0 fusion.5
  241.9 4.1 %multiply_reduce_fusion.1 = (f32[512,4]{0,1:T(4,128)S(1)}, f32[512,4,128]{0,2,1:T(8,128)}) fusion(f32[512,4,128]{0,2,1:T(8,128)} %fusion.5, f32[512,4]{0,1:T(4,128)S(1)} %copy-done.11, bf16[512,4,128]{0,2,1:T(8,128)(2,1)S(1)} %bitcast.126, f32[4,512]{1,0:T(4,128)S(1)} %bitcast.132, pred[512,512]{0,1:T(8,128)(4,1)S(1)} %fusion.48, ...), kind=kOutput, calls=%fused_computation.54 | convolution fusion | flops 543160320 | bytes 3956736 | tf_op jit(solution)/shard_map/while/body/eval_jaxpr/hqk,khd->qhd/dot_general | solution.py:109
  246.0 0.0 copy-start.4
  246.0 3.1 fusion.31
  249.1 2.1 fusion.93
  251.2 0.0 reduce-scatter.2.cloned.1.call-update
  251.2 0.0 copy-start.2
  251.2 0.0 all-gather.11.cloned.1.call-start
  251.3 0.5 all-gather.11.cloned.1.call-update
  251.8 11.9 %reduce-scatter.2.cloned.1.call-done = f32[256,1024]{1,0:T(8,128)} async-done(((f32[512,1024]{1,0:T(8,128)}), f32[256,1024]{1,0:T(8,128)}) %reduce-scatter.2.cloned.1.call-update) | async-done | bytes 1048592 | tf_op jit(solution)/shard_map/reduce_scatter | solution.py:117
  263.7 1.5 fusion.42
  265.2 36.4 %all-gather.11.cloned.1.call-done = bf16[3,1024,2816]{2,1,0:T(8,128)(2,1)} async-done(((bf16[3,1024,1408]{2,1,0:T(8,128)(2,1)}), bf16[3,1024,2816]{2,1,0:T(8,128)(2,1)}) %all-gather.11.cloned.1.call-update) | async-done | bytes 17301520 | tf_op jit(solution)/shard_map/all_gather | solution.py:125
  301.6 6.1 %fusion.7 = f32[2,256,2816]{2,1,0:T(8,128)S(1)} fusion(bf16[3,1024,2816]{2,1,0:T(8,128)(2,1)} %all-gather.11.cloned.1.call-done, bf16[256,1024]{1,0:T(8,128)(2,1)S(1)} %get-tuple-element.24, f32[1024]{0:T(1024)S(1)} %bitcast.133, f32[256]{0:T(256)S(1)} %add_rsqrt_fusion.1), kind=kOutput, calls=%fused_computation.10 | convolution fusion | flops 2953838592 | bytes 17830912 | tf_op jit(solution)/shard_map/td,kdf->ktf/dot_general | solution.py:126
  307.7 0.0 copy-start.1
  307.7 5.4 %fusion.32 = bf16[256,1024]{1,0:T(8,128)(2,1)} fusion(bf16[3,1024,2816]{2,1,0:T(8,128)(2,1)} %all-gather.11.cloned.1.call-done, f32[2,256,2816]{2,1,0:T(8,128)S(1)} %fusion.7, bf16[256,1024]{1,0:T(8,128)(2,1)} %copy-done.7), kind=kOutput, calls=%fused_computation.40 | convolution fusion | flops 1481506816 | bytes 12582912 | tf_op jit(solution)/shard_map/tf,df->td/dot_general | solution.py:130
  (34 shorter events, 0.1 us)
Async XLA Ops:
  6.5 32.3 %copy-start = (bf16[3,1024,512]{2,1,0:T(8,128)(2,1)S(1)}, bf16[3,1024,512]{2,1,0:T(8,128)(2,1)}, u32[]{:S(2)}) copy-start(bf16[3,1024,512]{2,1,0:T(8,128)(2,1)} %param.15) | copy-start | bytes 9437188
  6.5 20.3 %all-gather.5.cloned.1.call-start = ((), (), s32[]{:S(2)}) async-start(), calls=%async_computation.1 | async-start | bytes 1572864 | tf_op jit(solution)/shard_map/all_gather | solution.py:41
  11.3 33.5 %all-gather.7.cloned.1.call-start = ((), (), s32[]{:S(2)}) async-start(), calls=%async_computation.2 | async-start | bytes 3145728 | tf_op jit(solution)/shard_map/all_gather | solution.py:52
  12.1 195.6 %all-gather.9.cloned.1.call-start = ((), (), s32[]{:S(2)}) async-start(), calls=%async_computation.3 | async-start | bytes 34078720 | tf_op jit(solution)/shard_map/all_gather | solution.py:85
  12.8 250.9 %reduce-scatter.2.cloned.1.call-start = ((), (), s32[]{:S(2)}) async-start(), calls=%async_computation.4 | async-start | bytes 3145728 | tf_op jit(solution)/shard_map/reduce_scatter | solution.py:117
  28.5 0.6 copy-start.8
  38.9 3.4 %copy-start.9 = (f32[2,512,4]{1,2,0:T(4,128)S(1)}, f32[2,512,4]{1,2,0:T(4,128)}, u32[]{:S(2)}) copy-start(f32[2,512,4]{1,2,0:T(4,128)} %copy-done.8) | copy-start | bytes 49156
  38.9 3.4 %copy-start.16 = (f32[4]{0:T(128)S(1)}, f32[4]{0:T(128)}, u32[]{:S(2)}) copy-start(f32[4]{0:T(128)} %param.17) | copy-start | bytes 52
  38.9 3.5 %copy-start.10 = (f32[6,512]{1,0:T(8,128)S(1)}, f32[6,512]{1,0:T(8,128)}, u32[]{:S(2)}) copy-start(f32[6,512]{1,0:T(8,128)} %fusion.62) | copy-start | bytes 36868
  42.1 2.7 copy-start.15
  42.1 6.7 %copy-start.3 = (bf16[512,1024]{1,0:T(8,128)(2,1)S(1)}, bf16[512,1024]{1,0:T(8,128)(2,1)}, u32[]{:S(2)}) copy-start(bf16[512,1024]{1,0:T(8,128)(2,1)} %all-gather.5.cloned.1.call-done) | copy-start | bytes 3145732
  50.9 156.8 %copy-start.17 = (s32[1,6]{1,0:T(1,128)S(1)}, s32[1,6]{1,0:T(1,128)}, u32[]{:S(2)}) copy-start(s32[1,6]{1,0:T(1,128)} %param.22) | copy-start | bytes 76
  239.8 2.1 copy-start.5
  239.8 2.1 copy-start.6
  239.8 2.0 copy-start.11
  239.8 2.0 copy-start.12
  241.9 4.1 %copy-start.13 = (f32[512,4]{0,1:T(4,128)S(1)}, f32[512,4]{0,1:T(4,128)}, u32[]{:S(2)}) copy-start(f32[512,4]{0,1:T(4,128)} %fusion.69) | copy-start | bytes 24580
  246.0 3.1 copy-start.4
  251.2 12.5 %copy-start.2 = (bf16[256,1024]{1,0:T(8,128)(2,1)S(1)}, bf16[256,1024]{1,0:T(8,128)(2,1)}, u32[]{:S(2)}) copy-start(bf16[256,1024]{1,0:T(8,128)(2,1)} %param.13) | copy-start | bytes 1572868
  251.2 50.4 %copy-start.14 = (f32[1,1024]{1,0:T(1,128)S(1)}, f32[1,1024]{1,0:T(1,128)}, u32[]{:S(2)}) copy-start(f32[1,1024]{1,0:T(1,128)} %get-tuple-element.27) | copy-start | bytes 12292
  251.2 50.4 %all-gather.11.cloned.1.call-start = ((), (), s32[]{:S(2)}) async-start(), calls=%async_computation.5 | async-start | bytes 25952256 | tf_op jit(solution)/shard_map/all_gather | solution.py:125
  265.1 36.5 %copy-start.7 = (bf16[256,1024]{1,0:T(8,128)(2,1)}, bf16[256,1024]{1,0:T(8,128)(2,1)S(1)}, u32[]{:S(2)}) copy-start(bf16[256,1024]{1,0:T(8,128)(2,1)S(1)} %get-tuple-element.24) | copy-start | bytes 1572868
  307.7 5.4 %copy-start.1 = (bf16[3,1024,512]{2,1,0:T(8,128)(2,1)S(1)}, bf16[3,1024,512]{2,1,0:T(8,128)(2,1)}, u32[]{:S(2)}) copy-start(bf16[3,1024,512]{2,1,0:T(8,128)(2,1)} %param.15) | copy-start | bytes 9437188
Sparse Core Ops, SparseCore 0:
  11.5 15.3 all-gather.4
  28.5 14.6 all-gather.6
  46.0 161.6 all-gather.8
  251.3 12.3 reduce-scatter.1
  265.3 36.2 all-gather.10
where the time goes:
time: 320 us
  waiting for transfers between devices  211 us (66%)
  matrix products  72.2 us (23%)
  other arithmetic  14.3 us (4%)
  between operations  13.4 us (4%)
  local copies, waits for them, and re-layouts  8.44 us (3%)
    all_gather x1, waiting for transfers between devices, on_device(): token_segment = lax.all_gather(caches, 'req', axis=0, tiled=True)  152 us
    all_gather x1, waiting for transfers between devices, on_device(): lax.all_gather(feedforward_weight, 'col', axis=2, tiled=True)  36.4 us
    dot_general x1, matrix products, on_device(): jnp.einsum('sn,nhij->shij', select, token_segment, preferred_element_type...  32 us
    reduce_scatter x1, waiting for transfers between devices, on_device(): lax.psum_scatter(jnp.dot(head_out, head_output_weight, preferred_element_...  11.9 us
    all_gather x1, waiting for transfers between devices, on_device(): gathered = lax.all_gather(normalized_rows, 'col', axis=0, tiled=True)  8.81 us
  transfers between devices with their start and end apart: 5, of which 4 were waited for; matrix products, arithmetic and copies ran while one was open for 11% of the time, Pallas kernels for 0%

commit v1 on v0

v1 whole, which is shorter than its diff:
```python
import math

import jax
import jax.numpy as jnp
import numpy as np
from jax import lax
from jax.sharding import Mesh
from jax.sharding import PartitionSpec as P

epsilon = 1e-05
ROWS = ("z", "y", "x", "col")


def rms_scale(values, gain):
    widened = values.astype(jnp.float32)
    factor = lax.rsqrt(jnp.mean(widened * widened, axis=-1, keepdims=True) + epsilon)
    return (widened * factor * gain).astype(jnp.bfloat16)


def swap(value):
    return lax.ppermute(value, "col", perm=[(0, 1), (1, 0)])


def pair_rows(mine, other, col):
    first = jnp.where(col == 0, mine, other)
    second = jnp.where(col == 0, other, mine)
    return jnp.concatenate([first, second], axis=0)


def on_device(
    tokens,
    norm_gain_pair,
    query_key_value_weight,
    head_gate_weight,
    decay_logit_bias,
    adapter_down_factor,
    adapter_up_factor,
    lengths,
    request_adapter_index,
    request_cache_index,
    caches,
    head_output_weight,
    feedforward_weight,
):
    tok_rows, width = tokens.shape
    col = lax.axis_index("col")
    col_count = 2
    group = tok_rows * col_count
    head_cols = query_key_value_weight.shape[2]
    local_heads = head_gate_weight.shape[2]
    head_size = head_cols // local_heads
    group_lengths = lengths[0].reshape(-1)
    scale = 1.0 / math.sqrt(head_size)

    ff_other = swap(feedforward_weight)
    down_other = swap(adapter_down_factor)

    plane = lax.all_gather(caches, ("y", "x"), axis=0, tiled=True)
    per_plane = plane.shape[0]
    line_index = lax.all_gather(request_cache_index[0], "z", axis=0)
    local = line_index - lax.axis_index("z") * per_plane
    valid = (local >= 0) & (local < per_plane)
    picked = plane[jnp.clip(local, 0, per_plane - 1)]
    slots = jnp.where(valid[:, :, None, None, None], picked, jnp.zeros_like(picked))
    states = lax.psum_scatter(slots, "z", scatter_dimension=0, tiled=True)[0]

    normalized_rows = rms_scale(tokens, norm_gain_pair[0])
    gathered = pair_rows(normalized_rows, swap(normalized_rows), col)
    positions = jnp.arange(group, dtype=jnp.int32)
    ends = jnp.cumsum(group_lengths)
    starts = ends - group_lengths
    member = (
        (positions[:, None] >= starts[None, :]) & (positions[:, None] < ends[None, :])
    ).astype(jnp.float32)
    segment = jnp.sum((positions[:, None] >= ends[None, :]).astype(jnp.int32), axis=1)
    projected = jnp.einsum(
        "td,kdc->ktc", gathered, query_key_value_weight, preferred_element_type=jnp.float32
    )
    half_adapters = adapter_down_factor.shape[0]
    mine_numbers = col * half_adapters + jnp.arange(half_adapters, dtype=jnp.int32)
    other_numbers = (1 - col) * half_adapters + jnp.arange(half_adapters, dtype=jnp.int32)
    wanted = request_adapter_index[0][:, None]
    select_mine = (wanted == mine_numbers[None, :]).astype(jnp.bfloat16)
    select_other = (wanted == other_numbers[None, :]).astype(jnp.bfloat16)
    chosen = (
        jnp.einsum("sa,adr->sdr", select_mine, adapter_down_factor, preferred_element_type=jnp.float32)
        + jnp.einsum("sa,adr->sdr", select_other, down_other, preferred_element_type=jnp.float32)
    ).astype(jnp.bfloat16)
    per_request = jnp.einsum("td,sdr->tsr", gathered, chosen, preferred_element_type=jnp.float32)
    low_rank_delta = jnp.sum(member[:, :, None] * per_request, axis=1)
    low_rank_delta = low_rank_delta.astype(jnp.bfloat16)
    adapter_onehot = (
        request_adapter_index[0][:, None]
        == jnp.arange(adapter_up_factor.shape[0], dtype=jnp.int32)[None, :]
    ).astype(jnp.bfloat16)
    up_chosen = jnp.einsum(
        "gq,qjl->gjl", adapter_onehot, adapter_up_factor, preferred_element_type=jnp.float32
    ).astype(jnp.bfloat16)
    delta_all = jnp.einsum(
        "tr,src->tsc", low_rank_delta, up_chosen, preferred_element_type=jnp.float32
    )
    delta = jnp.sum(member[:, :, None] * delta_all, axis=1)
    queries = (projected[0] + delta).astype(jnp.bfloat16).reshape(group, local_heads, head_size)
    keys = projected[1].astype(jnp.bfloat16).reshape(group, local_heads, head_size)
    values = projected[2].astype(jnp.bfloat16).reshape(group, local_heads, head_size)
    gate_terms = jnp.einsum(
        "td,kdh->kth", gathered, head_gate_weight, preferred_element_type=jnp.float32
    )
    log_keep = jax.nn.log_sigmoid(gate_terms[0] + decay_logit_bias[None, :])
    mix_gate = jax.nn.sigmoid(gate_terms[1])
    running = jnp.cumsum(log_keep, axis=0)
    before = running - log_keep
    start_hot = (positions[None, :] == starts[:, None]).astype(jnp.float32)
    start_level = jnp.sum(start_hot[:, :, None] * before[None, :, :], axis=1)
    level = running - jnp.sum(member[:, :, None] * start_level[None, :, :], axis=1)
    from_state = jnp.einsum("thi,shij->tshj", queries, states, preferred_element_type=jnp.float32)
    carried = jnp.sum(member[:, :, None, None] * from_state, axis=1) * jnp.exp(level)[:, :, None]

    scores = jnp.einsum("qhd,khd->hqk", queries, keys, preferred_element_type=jnp.float32) * scale
    allowed = (segment[:, None] == segment[None, :]) & (positions[None, :] <= positions[:, None])
    masked = jnp.where(allowed[None], scores, -jnp.inf)
    peak = jnp.max(masked, axis=2, keepdims=True)
    weights = jnp.exp(masked - peak)
    probs = (weights / jnp.sum(weights, axis=2, keepdims=True)).astype(jnp.bfloat16)
    attended = jnp.einsum("hqk,khd->qhd", probs, values, preferred_element_type=jnp.float32)
    gap = jnp.where(allowed[None], running.T[:, :, None] - running.T[:, None, :], -jnp.inf)
    memory_w = (scores * jnp.exp(gap)).astype(jnp.bfloat16)
    recalled = jnp.einsum("hqk,khd->qhd", memory_w, values, preferred_element_type=jnp.float32)
    recalled = recalled + carried
    factor = lax.rsqrt(jnp.mean(recalled * recalled, axis=2, keepdims=True) + epsilon)
    combined = attended + mix_gate[:, :, None] * recalled * factor
    head_out = combined.astype(jnp.bfloat16).reshape(group, head_cols)

    partial = jnp.dot(head_out, head_output_weight, preferred_element_type=jnp.float32)
    own = lax.dynamic_slice_in_dim(partial, col * tok_rows, tok_rows, axis=0)
    sent = lax.dynamic_slice_in_dim(partial, (1 - col) * tok_rows, tok_rows, axis=0)
    attn_proj = own + swap(sent)
    mixed = (tokens.astype(jnp.float32) + attn_proj).astype(jnp.bfloat16)
    normed_two = rms_scale(mixed, norm_gain_pair[1])

    def feed_half(weight):
        gate_up = jnp.einsum(
            "td,kdf->ktf", normed_two, weight[:2], preferred_element_type=jnp.float32
        )
        hidden = (jax.nn.silu(gate_up[0]) * gate_up[1]).astype(jnp.bfloat16)
        return jnp.einsum("tf,df->td", hidden, weight[2], preferred_element_type=jnp.float32)

    feed = feed_half(feedforward_weight) + feed_half(ff_other)
    return (mixed.astype(jnp.float32) + feed).astype(jnp.bfloat16)


def solution(mesh):
    n_req = mesh.shape["req"]
    side = round(n_req ** (1.0 / 3.0))
    devices = np.asarray(mesh.devices).reshape(side, side, n_req // (side * side), mesh.shape["col"])
    grid = Mesh(devices, ROWS)
    placed = (
        P(ROWS, None),
        P(),
        P(None, None, "col"),
        P(None, None, "col"),
        P("col"),
        P("col", None, None),
        P(None, None, "col"),
        P(ROWS[:3], None, None),
        P(ROWS[:3], None),
        P(ROWS[:3], None),
        P(ROWS[:3], "col", None, None),
        P("col", None),
        P(None, None, "col"),
    )
    return jax.shard_map(
        on_device, mesh=grid, in_specs=placed, out_specs=P(ROWS, None), check_vma=False
    )
```

time: 320 us -> 178 us (0.56)
  waiting for transfers between devices: 211 us -> 67 us
  matrix products: 72.2 us -> 42.3 us
  local copies, waits for them, and re-layouts: 8.44 us -> 22.9 us
  blocking collectives: 0 us -> 10.1 us
  other arithmetic: 14.3 us -> 20 us
    all_gather x4 -> x1, waiting for transfers between devices: 197 us -> 63.2 us  [on_device(): plane = lax.all_gather(caches, ('y', 'x'), axis=0, tiled=True)]
    dot_general x6 -> x8, matrix products: 54.6 us -> 26.3 us  [the longest x2 8.73 us: feed_half(): jnp.einsum('td,kdf->ktf', normed_two, weight[:2], preferred_element_type=...]
    reduce_scatter x1, waiting for transfers between devices: 11.9 us -> 0.02 us  [on_device(): states = lax.psum_scatter(slots, 'z', scatter_dimension=0, tiled=True)[0]]
    gather x0 -> x2, local copies, waits for them, and re-layouts: none -> 10.9 us  [on_device(): picked = plane[jnp.clip(local, 0, per_plane - 1)]]
    all_gather x0 -> x1, blocking collectives: none -> 10.1 us  [on_device(): line_index = lax.all_gather(request_cache_index[0], 'z', axis=0)]
    select_n x0 -> x3, other arithmetic: none -> 5.37 us  [the longest x1 3.81 us: on_device(): jnp.where(valid[:, :, None, None, None], picked, jnp.zeros_like(picked))]
    unnamed x37 -> x53, local copies, waits for them, and re-layouts: 1.3 us -> 4.86 us
  transfers between devices with their start and end apart: 5 -> 6, of which waited for: 4 -> 2; matrix products, arithmetic and copies ran while one was open for 11% -> 34% of each run, Pallas kernels for 0% -> 0%
where the time goes in v1:
time: 178 us; the launch traced here: 177 us
  waiting for transfers between devices  67 us (38%)
  matrix products  42.3 us (24%)
  local copies, waits for them, and re-layouts  22.9 us (13%)
  other arithmetic  20 us (11%)
  between operations  13.8 us (8%)
  blocking collectives  10.1 us (6%)
    all_gather x1, waiting for transfers between devices, on_device(): plane = lax.all_gather(caches, ('y', 'x'), axis=0, tiled=True)  63.2 us
    gather x2, local copies, waits for them, and re-layouts, on_device(): picked = plane[jnp.clip(local, 0, per_plane - 1)]  10.9 us
    all_gather x1, blocking collectives, on_device(): line_index = lax.all_gather(request_cache_index[0], 'z', axis=0)  10.1 us
    dot_general x2, matrix products, feed_half(): jnp.einsum('td,kdf->ktf', normed_two, weight[:2], preferred_element_type=...  8.73 us
    dot_general x2, matrix products, feed_half(): jnp.einsum('tf,df->td', hidden, weight[2], preferred_element_type=jnp.flo...  6.71 us
    unnamed x53, local copies, waits for them, and re-layouts  4.86 us
    sub x1, matrix products, on_device(): weights = jnp.exp(masked - peak)  4.67 us
    another operation x3, other arithmetic  4.54 us
  transfers between devices with their start and end apart: 6, of which 2 were waited for; matrix products, arithmetic and copies ran while one was open for 34% of the time, Pallas kernels for 0%

profile of v1, /device:TPU:1, one launch (start us, length us, event | category | flops | bytes accessed | tf_op | source)
XLA Modules:
  0.0 177.2 jit_solution(17302642569815768344)
XLA Ops:
  6.5 0.7 all-gather.3.cloned.1.call-update
  7.3 0.0 reduce-scatter.2.cloned.1.call-start
  7.3 10.1 %all-gather = s32[4,1,6]{2,1,0:T(1,128)S(1)} all-gather(s32[1,1,6]{2,1,0:T(1,128)} %bitcast.159), channel_id=1, replica_groups=mesh['z'=4,'y'=4,'x'=4,'col'=2] {'z'}, dimensions={0}, use_global_device_ids=true | all-gather | bytes 120 | tf_op jit(solution)/shard_map/all_gather | solution.py:60
  17.4 0.1 reshape.282
  17.5 1.2 fusion.33
  18.7 1.4 fusion.95
  20.1 63.2 %all-gather.3.cloned.1.call-done = bf16[64,4,128,128]{3,2,1,0:T(8,128)(2,1)} async-done(((bf16[4,4,128,128]{3,2,1,0:T(8,128)(2,1)}), bf16[64,4,128,128]{3,2,1,0:T(8,128)(2,1)}) %all-gather.3.cloned.1.call-update) | async-done | bytes 8388624 | tf_op jit(solution)/shard_map/all_gather | solution.py:58
  83.4 6.2 %gather_fusion = bf16[24,4,128,128]{3,2,1,0:T(8,128)(2,1)} fusion(bf16[64,4,128,128]{3,2,1,0:T(8,128)(2,1)} %all-gather.3.cloned.1.call-done, s32[1024]{0:T(1024)S(1)} %pad_clamp_fusion), kind=kCustom, calls=%fused_computation | custom fusion | bytes 6291552 | tf_op jit(solution)/shard_map/gather | solution.py:63
  89.5 4.7 %copy.59 = bf16[4,6,4,128,128]{3,4,1,2,0:T(8,128)(2,1)} copy(bf16[4,6,4,128,128]{4,3,2,1,0:T(8,128)(2,1)} %bitcast.136) | data formatting | bytes 6291456 | tf_op jit(solution)/shard_map/gather | solution.py:63
  94.3 3.8 %broadcast_select_fusion = bf16[4,6,4,128,128]{3,4,1,2,0:T(8,128)(2,1)} fusion(bf16[4,6,4,128,128]{3,4,1,2,0:T(8,128)(2,1)} %copy.59, pred[4,6]{1,0:T(4,128)(4,1)S(1)} %bitcast.156), kind=kLoop, calls=%fused_computation.16 | loop fusion | flops 1572864 | bytes 6291480 | tf_op jit(solution)/shard_map/jit(_where)/select_n | solution.py:64
  98.1 0.0 reduce-scatter.2.cloned.1.call-update
  98.1 2.0 %fusion.35 = bf16[256,1024]{1,0:T(8,128)(2,1)} fusion(bf16[256,1024]{1,0:T(8,128)(2,1)} %param.13, f32[1024]{0:T(1024)S(1)} %bitcast.146, f32[256]{0:T(256)S(1)} %add_rsqrt_fusion.2), kind=kLoop, calls=%fused_computation.52 | loop fusion | flops 1048576 | bytes 1053696 | tf_op jit(solution)/shard_map/convert_element_type | solution.py:17
  100.2 0.7 collective-permute-start
  100.9 2.8 %copy.49 = bf16[32,1024,16]{1,0,2:T(8,128)(2,1)} copy(bf16[32,1024,16]{1,2,0:T(8,128)(2,1)} %param.18) | data formatting | bytes 2097152 | tf_op args[5]
  103.6 0.5 collective-permute-start.3
  104.1 0.1 reshape_squeeze.3
  104.2 0.1 reshape.275
  104.3 0.2 reduce-window.14
  104.5 0.5 iota_add_fusion.1
  105.0 0.1 convert_reduce_fusion
  105.1 0.7 fusion.61
  105.8 0.1 fusion.60
  105.8 0.2 fusion.43
  106.0 0.5 iota_add_fusion
  106.5 2.7 %convolution_convert_fusion = bf16[6,16,512]{2,0,1:T(8,128)(2,1)S(1)} fusion(bf16[64,16,512]{2,1,0:T(8,128)(2,1)} %param.19, s32[6]{0:T(128)} %bitcast.151), kind=kOutput, calls=%fused_computation.48 | convolution fusion | flops 6340992 | bytes 1146904 | tf_op jit(solution)/shard_map/gq,qjl->gjl/dot_general | solution.py:96
  109.3 3.2 %fusion.73 = f32[6,1024,16]{1,0,2:T(8,128)} fusion(s32[32]{0:T(128)} %iota_add_fusion.1, s32[6]{0:T(128)} %bitcast.152, bf16[32,1024,16]{1,2,0:T(8,128)(2,1)} %param.18), kind=kOutput, calls=%fused_computation.111 | convolution fusion | flops 6291648 | bytes 1441944 | tf_op jit(solution)/shard_map/sa,adr->sdr/dot_general | solution.py:86
  112.5 1.6 broadcast_select_fusion.2
  114.1 0.8 copy-done.5
  114.9 1.1 convolution_bitcast_fusion.1
  116.0 0.6 copy-done.13
  116.6 0.7 fusion.91
  117.3 1.3 reshape.277
  118.6 3.0 %reduce-window.18 = f32[4,4,128]{2,1,0:T(4,128)} reduce-window(f32[4,4,128]{2,1,0:T(4,128)} %reshape.277, f32[]{:T(128)} %constant.20.clone.1), window={size=1x1x128 pad=0_0x0_0x127_0}, to_apply=%region_7.8 | reduce-window | flops 260096 | bytes 16388 | tf_op jit(solution)/shard_map/reduce-window.1
  121.6 1.4 slice_reduce_fusion
  123.0 1.3 reduce-window.19
  124.4 0.8 add_bitcast_fusion
  125.2 3.1 %fusion.96 = (bf16[3,512,512]{1,2,0:T(8,128)(2,1)S(1)}, f32[3,512,512]{1,2,0:T(8,128)S(1)}) fusion(bf16[3,1024,512]{2,1,0:T(8,128)(2,1)S(1)} %copy-done, bf16[256,1024]{1,0:T(8,128)(2,1)} %copy-done.7, bf16[256,1024]{1,0:T(8,128)(2,1)} %copy-done.5), kind=kOutput, calls=%fused_computation.141 | convolution fusion | flops 1613496320 | bytes 8912896 | tf_op jit(solution)/shard_map/td,kdc->ktc/dot_general | solution.py:76
  128.3 0.1 bitcast_subtract_fusion.1
  128.4 0.6 copy.83
  129.0 0.1 slice.73
  129.1 0.1 multiply_reduce_fusion.4
  129.2 0.1 multiply_reduce_fusion.3
  129.3 0.6 fusion.68
  129.9 0.6 fusion.69
  130.5 1.1 fusion.94
  131.6 1.6 fusion.32
  133.1 0.1 copy.51
  133.3 0.5 fusion.53
  133.8 1.0 multiply_reduce_fusion
  134.8 0.3 copy.54
  135.1 0.3 add_convert_fusion
  135.4 4.7 %fusion.97 = (f32[4,512]{1,0:T(4,128)S(1)}, f32[4,512,512]{1,2,0:T(8,128)}) fusion(pred[512,512]{0,1:T(8,128)(4,1)S(1)} %fusion.43, bf16[512,4,128]{0,2,1:T(8,128)(2,1)S(1)} %add_convert_fusion, bf16[512,4,128]{0,2,1:T(8,128)(2,1)} %bitcast.142), kind=kOutput, calls=%fused_computation.142 | convolution fusion | flops 272630272 | bytes 5513216 | tf_op jit(solution)/shard_map/sub | solution.py:123
  140.1 0.0 reduce-scatter.2.cloned.1.call-done
  140.1 2.2 %fusion.1 = f32[512,4,128]{0,2,1:T(8,128)S(1)} fusion(f32[512,6]{0,1:T(8,128)S(1)} %fusion.60, bf16[1,6,4,128,128]{3,4,1,2,0:T(8,128)(2,1)} %reduce-scatter.2.cloned.1.call-done, bf16[512,4,128]{0,2,1:T(8,128)(2,1)S(1)} %add_convert_fusion), kind=kOutput, calls=%fused_computation.3 | convolution fusion | flops 405536768 | bytes 2371584 | tf_op jit(solution)/shard_map/thi,shij->tshj/dot_general | solution.py:116
  142.4 2.9 %multiply_reduce_fusion.1 = (f32[512,4]{0,1:T(4,128)S(1)}, f32[512,4,128]{0,2,1:T(8,128)}) fusion(f32[512,4,128]{0,2,1:T(8,128)S(1)} %fusion.1, f32[512,4]{0,1:T(4,128)S(1)} %copy-done.16, bf16[512,4,128]{0,2,1:T(8,128)(2,1)S(1)} %bitcast.140, f32[4,512]{1,0:T(4,128)S(1)} %bitcast.149, pred[512,512]{0,1:T(8,128)(4,1)S(1)} %fusion.43, ...), kind=kOutput, calls=%fused_computation.61 | convolution fusion | flops 543160320 | bytes 3956736 | tf_op jit(solution)/shard_map/hqk,khd->qhd/dot_general | solution.py:128
  145.3 3.1 %fusion.30 = bf16[512,4,128]{0,2,1:T(8,128)(2,1)S(1)} fusion(bf16[512,4,128]{0,2,1:T(8,128)(2,1)S(1)} %bitcast.141, f32[4,512,512]{1,2,0:T(8,128)} %get-tuple-element.16, f32[4,512]{1,0:T(4,128)S(1)} %get-tuple-element.15, f32[512,4,128]{0,2,1:T(8,128)} %get-tuple-element.18, f32[512,4]{0,1:T(4,128)S(1)} %add_rsqrt_fusion, f32[512,4]{0,1:T(4,128)S(1)} %copy-done.17), kind=kOutput, calls=%fused_computation.44 | convolution fusion | flops 271581184 | bytes 6316032 | tf_op jit(solution)/shard_map/hqk,khd->qhd/dot_general | solution.py:125
  148.5 0.7 fusion.100
  149.2 1.2 constant_dynamic-slice_fusion
  150.4 3.0 %collective-permute-done.2 = f32[256,1024]{1,0:T(8,128)} collective-permute-done((f32[256,1024]{1,0:T(8,128)}, f32[256,1024]{1,0:T(8,128)}, u32[]{:S(2)}, u32[]{:S(2)}) %collective-permute-start.2) | collective-permute-done | bytes 1048608 | tf_op jit(solution)/shard_map/ppermute | solution.py:21
  153.4 1.5 fusion.37
  154.9 4.4 %fusion.6 = f32[2,256,1408]{2,1,0:T(8,128)S(1)} fusion(bf16[3,1024,1408]{2,1,0:T(8,128)(2,1)} %param.25, bf16[256,1024]{1,0:T(8,128)(2,1)S(1)} %get-tuple-element.6, f32[1024]{0:T(1024)S(1)} %bitcast.154, f32[256]{0:T(256)S(1)} %add_rsqrt_fusion.1), kind=kOutput, calls=%fused_computation.13 | convolution fusion | flops 1477443584 | bytes 9180160 | tf_op jit(solution)/shard_map/td,kdf->ktf/dot_general | solution.py:142
  159.3 2.9 %fusion.14 = f32[256,1024]{1,0:T(8,128)S(1)} fusion(bf16[3,1024,1408]{2,1,0:T(8,128)(2,1)} %param.25, f32[2,256,1408]{2,1,0:T(8,128)S(1)} %fusion.6), kind=kOutput, calls=%fused_computation.19 | convolution fusion | flops 740360192 | bytes 6815744 | tf_op jit(solution)/shard_map/tf,df->td/dot_general | solution.py:146
  162.2 4.4 %fusion.9 = f32[2,256,1408]{2,1,0:T(8,128)S(1)} fusion(bf16[3,1024,1408]{2,1,0:T(8,128)(2,1)} %collective-permute-done.3, bf16[256,1024]{1,0:T(8,128)(2,1)S(1)} %get-tuple-element.6, f32[1024]{0:T(1024)S(1)} %bitcast.155, f32[256]{0:T(256)S(1)} %add_rsqrt_fusion.1), kind=kOutput, calls=%fused_computation.14 | convolution fusion | flops 1477443584 | bytes 9180160 | tf_op jit(solution)/shard_map/td,kdf->ktf/dot_general | solution.py:142
  166.5 3.8 %fusion.31 = bf16[256,1024]{1,0:T(8,128)(2,1)} fusion(f32[256,1024]{1,0:T(8,128)S(1)} %fusion.14, bf16[3,1024,1408]{2,1,0:T(8,128)(2,1)} %collective-permute-done.3, bf16[256,1024]{1,0:T(8,128)(2,1)S(1)} %get-tuple-element.6, f32[2,256,1408]{2,1,0:T(8,128)S(1)} %fusion.9), kind=kOutput, calls=%fused_computation.45 | convolution fusion | flops 741408768 | bytes 7864320 | tf_op jit(solution)/shard_map/tf,df->td/dot_general | solution.py:146
  (64 shorter events, 0.2 us)
Async XLA Ops:
  6.5 118.6 %copy-start = (bf16[3,1024,512]{2,1,0:T(8,128)(2,1)S(1)}, bf16[3,1024,512]{2,1,0:T(8,128)(2,1)}, u32[]{:S(2)}) copy-start(bf16[3,1024,512]{2,1,0:T(8,128)(2,1)} %param.15) | copy-start | bytes 9437188
  6.5 76.8 %all-gather.3.cloned.1.call-start = ((), (), s32[]{:S(2)}) async-start(), calls=%async_computation.1 | async-start | bytes 8912896 | tf_op jit(solution)/shard_map/all_gather | solution.py:58
  7.3 132.8 %reduce-scatter.2.cloned.1.call-start = ((), (), s32[]{:S(2)}) async-start(), calls=%async_computation.2 | async-start | bytes 3932160 | tf_op jit(solution)/shard_map/reduce_scatter | solution.py:65
  20.1 78.0 %copy-start.12 = (f32[1,1024]{1,0:T(1,128)}, f32[1,1024]{1,0:T(1,128)S(1)}, u32[]{:S(2)}) copy-start(f32[1,1024]{1,0:T(1,128)S(1)} %get-tuple-element.12) | copy-start | bytes 12292
  98.1 6.0 %copy-start.24 = (s32[1,2,3]{2,1,0:T(2,128)S(1)}, s32[1,2,3]{2,1,0:T(2,128)}, u32[]{:S(2)}) copy-start(s32[1,2,3]{2,1,0:T(2,128)} %param.20) | copy-start | bytes 76
  98.1 2.0 %copy-start.15 = (f32[256]{0:T(256)}, f32[256]{0:T(256)S(1)}, u32[]{:S(2)}) copy-start(f32[256]{0:T(256)S(1)} %add_rsqrt_fusion.2) | copy-start | bytes 3076
  100.2 12.4 %collective-permute-start = (bf16[256,1024]{1,0:T(8,128)(2,1)}, bf16[256,1024]{1,0:T(8,128)(2,1)}, u32[]{:S(2)}, u32[]{:S(2)}) collective-permute-start(bf16[256,1024]{1,0:T(8,128)(2,1)} %fusion.35), channel_id=1, source_target_pairs={{0,1},{1,0},{2,3},{3,2},{4,5},{5,4},{6,7},{7,6},{8,9},{9,8},{10,11... | collective-permute-start | bytes 1572872 | tf_op jit(solution)/shard_map/ppermute | solution.py:21
  103.6 27.9 %collective-permute-start.1 = (bf16[32,1024,16]{1,0,2:T(8,128)(2,1)}, bf16[32,1024,16]{1,0,2:T(8,128)(2,1)}, u32[]{:S(2)}, u32[]{:S(2)}) collective-permute-start(bf16[32,1024,16]{1,0,2:T(8,128)(2,1)} %copy.49), channel_id=1, source_target_pairs={{0,1},{1,0},{2,3},{3,2},{4,5},{5,4},{6,7},{7,6},{8,9},{9,8},{10,11... | collective-permute-start | bytes 3145736 | tf_op jit(solution)/shard_map/ppermute | solution.py:21
  103.6 58.5 %collective-permute-start.3 = (bf16[3,1024,1408]{2,1,0:T(8,128)(2,1)}, bf16[3,1024,1408]{2,1,0:T(8,128)(2,1)}, u32[]{:S(2)}, u32[]{:S(2)}) collective-permute-start(bf16[3,1024,1408]{2,1,0:T(8,128)(2,1)} %param.25), channel_id=1, source_target_pairs={{0,1},{1,0},{2,3},{3,2},{4,5},{5,4},{6,7},{7,6},{8,9},{9,8},{10,11... | collective-permute-start | bytes 25952264 | tf_op jit(solution)/shard_map/ppermute | solution.py:21
  106.5 10.1 %copy-start.21 = (f32[4]{0:T(128)S(1)}, f32[4]{0:T(128)}, u32[]{:S(2)}) copy-start(f32[4]{0:T(128)} %param.17) | copy-start | bytes 52
  114.1 0.8 copy-start.5
  114.1 1.9 %copy-start.7 = (bf16[256,1024]{1,0:T(8,128)(2,1)}, bf16[256,1024]{1,0:T(8,128)(2,1)S(1)}, u32[]{:S(2)}) copy-start(bf16[256,1024]{1,0:T(8,128)(2,1)S(1)} %get-tuple-element.10) | copy-start | bytes 1572868
  116.0 0.6 copy-start.13
  125.1 3.1 %copy-start.14 = (f32[2,512,4]{1,2,0:T(4,128)S(1)}, f32[2,512,4]{1,2,0:T(4,128)}, u32[]{:S(2)}) copy-start(f32[2,512,4]{1,2,0:T(4,128)} %copy-done.13) | copy-start | bytes 49156
  125.1 3.1 %copy-start.22 = (f32[4]{0:T(128)S(1)}, f32[4]{0:T(128)}, u32[]{:S(2)}) copy-start(f32[4]{0:T(128)} %param.17) | copy-start | bytes 52
  125.1 3.9 %copy-start.11 = (f32[6,512]{1,0:T(8,128)S(1)}, f32[6,512]{1,0:T(8,128)}, u32[]{:S(2)}) copy-start(f32[6,512]{1,0:T(8,128)} %fusion.61) | copy-start | bytes 36868
  128.3 3.3 %copy-start.3 = (f32[6,1024,16]{1,0,2:T(8,128)S(1)}, f32[6,1024,16]{1,0,2:T(8,128)}, u32[]{:S(2)}) copy-start(f32[6,1024,16]{1,0,2:T(8,128)} %fusion.73) | copy-start | bytes 1179652
  128.3 3.3 %copy-start.19 = (s32[1,6]{1,0:T(1,128)S(1)}, s32[1,6]{1,0:T(1,128)}, u32[]{:S(2)}) copy-start(s32[1,6]{1,0:T(1,128)} %param.21) | copy-start | bytes 76
  128.3 3.3 %copy-start.23 = (s32[32]{0:T(128)S(1)}, s32[32]{0:T(128)}, u32[]{:S(2)}) copy-start(s32[32]{0:T(128)} %iota_add_fusion) | copy-start | bytes 388
  129.0 4.3 %copy-start.6 = (bf16[256,1024]{1,0:T(8,128)(2,1)S(1)}, bf16[256,1024]{1,0:T(8,128)(2,1)}, u32[]{:S(2)}) copy-start(bf16[256,1024]{1,0:T(8,128)(2,1)} %copy-done.5) | copy-start | bytes 1572868
  129.0 4.3 %copy-start.8 = (bf16[256,1024]{1,0:T(8,128)(2,1)S(1)}, bf16[256,1024]{1,0:T(8,128)(2,1)}, u32[]{:S(2)}) copy-start(bf16[256,1024]{1,0:T(8,128)(2,1)} %copy-done.7) | copy-start | bytes 1572868
  140.1 2.3 %copy-start.9 = (bf16[1,512,512]{1,2,0:T(8,128)(2,1)S(1)}, bf16[1,512,512]{1,2,0:T(8,128)(2,1)}, u32[]{:S(2)}) copy-start(bf16[1,512,512]{1,2,0:T(8,128)(2,1)} %get-tuple-element.8) | copy-start | bytes 1572868
  140.1 2.3 %copy-start.10 = (bf16[1,512,512]{1,2,0:T(8,128)(2,1)S(1)}, bf16[1,512,512]{1,2,0:T(8,128)(2,1)}, u32[]{:S(2)}) copy-start(bf16[1,512,512]{1,2,0:T(8,128)(2,1)} %get-tuple-element.7) | copy-start | bytes 1572868
  140.1 2.3 %copy-start.16 = (f32[512,4]{0,1:T(4,128)S(1)}, f32[512,4]{0,1:T(4,128)}, u32[]{:S(2)}) copy-start(f32[512,4]{0,1:T(4,128)} %fusion.69) | copy-start | bytes 24580
  140.1 2.3 %copy-start.18 = (f32[1,4,4,128]{3,1,2,0:T(4,128)S(1)}, f32[1,4,4,128]{3,1,2,0:T(4,128)}, u32[]{:S(2)}) copy-start(f32[1,4,4,128]{3,1,2,0:T(4,128)} %copy.83) | copy-start | bytes 24580
  142.4 2.9 %copy-start.17 = (f32[512,4]{0,1:T(4,128)S(1)}, f32[512,4]{0,1:T(4,128)}, u32[]{:S(2)}) copy-start(f32[512,4]{0,1:T(4,128)} %fusion.68) | copy-start | bytes 24580
  145.3 3.1 %copy-start.4 = (bf16[512,1024]{1,0:T(8,128)(2,1)S(1)}, bf16[512,1024]{1,0:T(8,128)(2,1)}, u32[]{:S(2)}) copy-start(bf16[512,1024]{1,0:T(8,128)(2,1)} %param.24) | copy-start | bytes 3145732
  148.4 5.0 %copy-start.2 = (bf16[256,1024]{1,0:T(8,128)(2,1)S(1)}, bf16[256,1024]{1,0:T(8,128)(2,1)}, u32[]{:S(2)}) copy-start(bf16[256,1024]{1,0:T(8,128)(2,1)} %param.13) | copy-start | bytes 1572868
  149.2 5.7 %copy-start.20 = (f32[1,1024]{1,0:T(1,128)S(1)}, f32[1,1024]{1,0:T(1,128)}, u32[]{:S(2)}) copy-start(f32[1,1024]{1,0:T(1,128)} %get-tuple-element.11) | copy-start | bytes 12292
  150.4 3.0 %collective-permute-start.2 = (f32[256,1024]{1,0:T(8,128)}, f32[256,1024]{1,0:T(8,128)}, u32[]{:S(2)}, u32[]{:S(2)}) collective-permute-start(f32[256,1024]{1,0:T(8,128)} %constant_dynamic-slice_fusion), channel_id=1, source_target_pairs={{0,1},{1,0},{2,3},{3,2},{4,5},{5,4},{6,7},{7,6},{8,9},{9,8},{10,11... | collective-permute-start | bytes 3145736 | tf_op jit(solution)/shard_map/ppermute | solution.py:21
  166.5 3.9 %copy-start.1 = (bf16[3,1024,512]{2,1,0:T(8,128)(2,1)S(1)}, bf16[3,1024,512]{2,1,0:T(8,128)(2,1)}, u32[]{:S(2)}) copy-start(bf16[3,1024,512]{2,1,0:T(8,128)(2,1)} %param.15) | copy-start | bytes 9437188
Sparse Core Ops, SparseCore 0:
  9.5 73.8 all-gather.2
  98.2 38.2 reduce-scatter.1

commit v2 on v1

--- a/solution.py
+++ b/solution.py
@@ -57,12 +57,33 @@
 
     plane = lax.all_gather(caches, ("y", "x"), axis=0, tiled=True)
     per_plane = plane.shape[0]
-    line_index = lax.all_gather(request_cache_index[0], "z", axis=0)
-    local = line_index - lax.axis_index("z") * per_plane
-    valid = (local >= 0) & (local < per_plane)
-    picked = plane[jnp.clip(local, 0, per_plane - 1)]
-    slots = jnp.where(valid[:, :, None, None, None], picked, jnp.zeros_like(picked))
-    states = lax.psum_scatter(slots, "z", scatter_dimension=0, tiled=True)[0]
+    z_count = lax.axis_size("z")
+    z_here = lax.axis_index("z")
+    own_index = request_cache_index[0]
+    shifts = range(1, z_count)
+    shifted = {
+        d: lax.ppermute(own_index, "z", perm=[(i, (i + d) % z_count) for i in range(z_count)])
+        for d in shifts
+    }
+
+    def pick(index_row):
+        local = index_row - z_here * per_plane
+        valid = (local >= 0) & (local < per_plane)
+        parts = []
+        for j in range(index_row.shape[0]):
+            one = lax.dynamic_index_in_dim(plane, jnp.clip(local[j], 0, per_plane - 1), 0, keepdims=False)
+            parts.append(jnp.where(valid[j], one, jnp.zeros_like(one)))
+        return jnp.stack(parts)
+
+    ahead = {d: None for d in shifts}
+    for d in shifts:
+        ahead[d] = shifted[z_count - d]
+    states = pick(own_index).astype(jnp.float32)
+    for d in shifts:
+        sent = pick(ahead[d])
+        got = lax.ppermute(sent, "z", perm=[(i, (i + d) % z_count) for i in range(z_count)])
+        states = states + got.astype(jnp.float32)
+    states = states.astype(jnp.bfloat16)
 
     normalized_rows = rms_scale(tokens, norm_gain_pair[0])
     gathered = pair_rows(normalized_rows, swap(normalized_rows), col)

time: 178 us -> 191 us (1.073)
  waiting for transfers between devices: 67 us -> 39.9 us
  other arithmetic: 20 us -> 44.3 us
  between operations: 13.8 us -> 29 us
  starting transfers between devices: 1.23 us -> 13.8 us
  blocking collectives: 10.1 us -> 0 us
  local copies, waits for them, and re-layouts: 22.9 us -> 17 us
  matrix products: 42.3 us -> 45.1 us
    all_gather x1, waiting for transfers between devices: 63.2 us -> 10.1 us  [on_device(): plane = lax.all_gather(caches, ('y', 'x'), axis=0, tiled=True)]
    ppermute x0 -> x6, waiting for transfers between devices: none -> 26.5 us  [the longest x3 26.4 us: on_device(): lax.ppermute(sent, 'z', perm=[(i, (i + d) % z_count) for i in range(z_cou...]
    unnamed x1 -> x6, other arithmetic: 0.77 us -> 23.1 us
    gather x2 -> x0, local copies, waits for them, and re-layouts: 10.9 us -> none  [on_device(): picked = plane[jnp.clip(local, 0, per_plane - 1)]]
    ppermute x0 -> x6, starting transfers between devices: none -> 10.2 us  [the longest x3 5.36 us: on_device(): lax.ppermute(own_index, 'z', perm=[(i, (i + d) % z_count) for i in range(...]
    all_gather x1 -> x0, blocking collectives: 10.1 us -> none  [on_device(): line_index = lax.all_gather(request_cache_index[0], 'z', axis=0)]
    slice x1 -> x9, local copies, waits for them, and re-layouts: 1.4 us -> 6.85 us  [the longest x4 2.7 us: pick(): local[j]]
    another operation x3 -> x4, other arithmetic: 4.54 us -> 9.19 us
  transfers between devices with their start and end apart: 6 -> 11, of which waited for: 2 -> 4; matrix products, arithmetic and copies ran while one was open for 34% -> 51% of each run, Pallas kernels for 0% -> 0%
where the time goes in v2:
time: 191 us; the launch traced here: 189 us
  matrix products  45.1 us (24%)
  other arithmetic  44.3 us (23%)
  waiting for transfers between devices  39.9 us (21%)
  between operations  29 us (15%)
  local copies, waits for them, and re-layouts  17 us (9%)
  starting transfers between devices  13.8 us (7%)
    ppermute x3, waiting for transfers between devices, on_device(): lax.ppermute(sent, 'z', perm=[(i, (i + d) % z_count) for i in range(z_cou...  26.4 us
    unnamed x6, other arithmetic  23.1 us
    all_gather x1, waiting for transfers between devices, on_device(): plane = lax.all_gather(caches, ('y', 'x'), axis=0, tiled=True)  10.1 us
    dot_general x2, matrix products, feed_half(): jnp.einsum('td,kdf->ktf', normed_two, weight[:2], preferred_element_type=...  8.73 us
    dot_general x2, matrix products, feed_half(): jnp.einsum('tf,df->td', hidden, weight[2], preferred_element_type=jnp.flo...  6.71 us
    unnamed x66, local copies, waits for them, and re-layouts  5.46 us
    ppermute x3, starting transfers between devices, on_device(): lax.ppermute(own_index, 'z', perm=[(i, (i + d) % z_count) for i in range(...  5.36 us
    ppermute x3, starting transfers between devices, on_device(): lax.ppermute(sent, 'z', perm=[(i, (i + d) % z_count) for i in range(z_cou...  4.83 us
  transfers between devices with their start and end apart: 11, of which 4 were waited for; matrix products, arithmetic and copies ran while one was open for 51% of the time, Pallas kernels for 0%

profile of v2, /device:TPU:1, one launch (start us, length us, event | category | flops | bytes accessed | tf_op | source)
XLA Modules:
  0.0 189.2 jit_solution(1232710678876782029)
XLA Ops:
  6.6 0.7 all-gather.2.cloned.1.call-update
  7.3 4.7 %collective-permute-start.2 = (s32[6]{0:T(128)}, s32[6]{0:T(128)}, u32[]{:S(2)}, u32[]{:S(2)}) collective-permute-start(s32[6]{0:T(128)} %bitcast.196), channel_id=1, source_target_pairs={{0,96},{32,0},{64,32},{96,64},{1,97},{33,1},{65,33},{97,65},{2,98}... | collective-permute-start | bytes 80 | tf_op jit(solution)/shard_map/ppermute | solution.py:65
  11.9 0.7 collective-permute-start.6
  12.6 2.8 %copy.49 = bf16[32,1024,16]{1,0,2:T(8,128)(2,1)} copy(bf16[32,1024,16]{1,2,0:T(8,128)(2,1)} %param.18) | data formatting | bytes 2097152 | tf_op args[5]
  15.4 1.5 collective-permute-start.1
  16.9 1.2 fusion.32
  18.2 0.6 fusion.94
  19.3 2.0 %fusion.34 = bf16[256,1024]{1,0:T(8,128)(2,1)} fusion(bf16[256,1024]{1,0:T(8,128)(2,1)} %param.13, f32[1024]{0:T(1024)S(1)} %bitcast.185, f32[256]{0:T(256)S(1)} %add_rsqrt_fusion.2), kind=kLoop, calls=%fused_computation.50 | loop fusion | flops 1048576 | bytes 1053696 | tf_op jit(solution)/shard_map/convert_element_type | solution.py:17
  21.6 0.7 fusion.96
  26.8 0.7 fusion.95
  27.6 0.7 fusion.60
  28.6 2.5 %convolution_convert_fusion = bf16[6,16,512]{2,0,1:T(8,128)(2,1)S(1)} fusion(bf16[64,16,512]{2,1,0:T(8,128)(2,1)} %param.19, s32[6]{0:T(128)} %bitcast.189), kind=kOutput, calls=%fused_computation.46 | convolution fusion | flops 6340992 | bytes 1146904 | tf_op jit(solution)/shard_map/gq,qjl->gjl/dot_general | solution.py:117
  31.0 3.2 %fusion.72 = f32[6,1024,16]{1,0,2:T(8,128)} fusion(s32[32]{0:T(128)S(1)} %iota_add_fusion.1, s32[6]{0:T(128)} %bitcast.190, bf16[32,1024,16]{1,2,0:T(8,128)(2,1)} %param.18), kind=kOutput, calls=%fused_computation.132 | convolution fusion | flops 6291648 | bytes 1441944 | tf_op jit(solution)/shard_map/sa,adr->sdr/dot_general | solution.py:107
  34.8 0.6 compare_and_fusion.2
  35.4 0.7 fusion.98
  36.6 0.7 compare_and_fusion.1
  37.3 0.6 compare_and_fusion
  37.9 0.7 fusion.100
  39.3 0.7 fusion.102
  50.0 0.7 fusion.97
  50.7 0.7 fusion.99
  51.4 0.7 fusion.101
  52.1 1.4 broadcast_select_fusion.1
  53.4 0.8 copy-done.8
  54.2 1.1 convolution_bitcast_fusion.1
  55.3 0.6 copy-done.15
  55.9 0.7 fusion.90
  56.6 1.3 reshape.372
  57.9 3.1 %reduce-window.18 = f32[4,4,128]{2,1,0:T(4,128)} reduce-window(f32[4,4,128]{2,1,0:T(4,128)} %reshape.372, f32[]{:T(128)} %constant.164.clone.1), window={size=1x1x128 pad=0_0x0_0x127_0}, to_apply=%region_7.8 | reduce-window | flops 260096 | bytes 16388 | tf_op jit(solution)/shard_map/reduce-window.1
  61.0 1.4 slice_reduce_fusion
  62.5 1.4 reduce-window.19
  63.9 0.8 add_bitcast_fusion
  64.7 3.1 %fusion.103 = (bf16[3,512,512]{1,2,0:T(8,128)(2,1)S(1)}, f32[3,512,512]{1,2,0:T(8,128)S(1)}) fusion(bf16[3,1024,512]{2,1,0:T(8,128)(2,1)S(1)} %copy-done, bf16[256,1024]{1,0:T(8,128)(2,1)} %copy-done.10, bf16[256,1024]{1,0:T(8,128)(2,1)} %copy-done.8), kind=kOutput, calls=%fused_computation.175 | convolution fusion | flops 1613496320 | bytes 8912896 | tf_op jit(solution)/shard_map/td,kdc->ktc/dot_general | solution.py:97
  68.0 0.6 copy.85
  68.8 0.6 fusion.67
  69.4 0.6 fusion.68
  70.0 1.1 fusion.93
  71.1 1.5 fusion.31
  73.3 10.1 %all-gather.2.cloned.1.call-done = bf16[64,4,128,128]{3,2,1,0:T(8,128)(2,1)} async-done(((bf16[4,4,128,128]{3,2,1,0:T(8,128)(2,1)}), bf16[64,4,128,128]{3,2,1,0:T(8,128)(2,1)}) %all-gather.2.cloned.1.call-update) | async-done | bytes 8388624 | tf_op jit(solution)/shard_map/all_gather | solution.py:58
  83.4 4.4 %select_dynamic-update-slice_fusion.23 = (bf16[6,4,128,128]{3,2,1,0:T(8,128)(2,1)S(1)}, bf16[6,4,128,128]{3,2,1,0:T(8,128)(2,1)}, bf16[6,4,128,128]{3,2,1,0:T(8,128)(2,1)}, bf16[6,4,128,128]{3,2,1,0:T(8,128)(2,1)}) fusion(bf16[64,4,128,128]{3,2,1,0:T(8,128)(2,1)} %all-gather.2.cloned.1.call-done, s32[]{:T(128)} %bitcast.24, pred[]{:T(512)} %bitcast.23, ...), kind=kLoop, calls=%fused_computation.97 | loop fusion | flops 262140 | bytes 1048596
  87.8 4.6 %select_dynamic-update-slice_fusion.22 = (bf16[6,4,128,128]{3,2,1,0:T(8,128)(2,1)S(1)}, bf16[6,4,128,128]{3,2,1,0:T(8,128)(2,1)}, bf16[6,4,128,128]{3,2,1,0:T(8,128)(2,1)}, bf16[6,4,128,128]{3,2,1,0:T(8,128)(2,1)}) fusion(bf16[6,4,128,128]{3,2,1,0:T(8,128)(2,1)S(1)} %get-tuple-element.35, bf16[64,4,128,128]{3,2,1,0:T(8,128)(2,1)} %all-gather.2.cloned.1.call-done, ...), kind=kLoop, calls=%fused_computation.96 | loop fusion | flops 262144 | bytes 1052672
  92.4 4.4 %select_dynamic-update-slice_fusion.21 = (bf16[6,4,128,128]{3,2,1,0:T(8,128)(2,1)S(1)}, bf16[6,4,128,128]{3,2,1,0:T(8,128)(2,1)}, bf16[6,4,128,128]{3,2,1,0:T(8,128)(2,1)}, bf16[6,4,128,128]{3,2,1,0:T(8,128)(2,1)}) fusion(bf16[6,4,128,128]{3,2,1,0:T(8,128)(2,1)S(1)} %get-tuple-element.31, bf16[64,4,128,128]{3,2,1,0:T(8,128)(2,1)} %all-gather.2.cloned.1.call-done, ...), kind=kLoop, calls=%fused_computation.95 | loop fusion | flops 262144 | bytes 1052672
  96.8 4.5 %select_dynamic-update-slice_fusion.20 = (bf16[6,4,128,128]{3,2,1,0:T(8,128)(2,1)S(1)}, bf16[6,4,128,128]{3,2,1,0:T(8,128)(2,1)}, bf16[6,4,128,128]{3,2,1,0:T(8,128)(2,1)}, bf16[6,4,128,128]{3,2,1,0:T(8,128)(2,1)}) fusion(bf16[6,4,128,128]{3,2,1,0:T(8,128)(2,1)S(1)} %get-tuple-element.27, bf16[64,4,128,128]{3,2,1,0:T(8,128)(2,1)} %all-gather.2.cloned.1.call-done, ...), kind=kLoop, calls=%fused_computation.94 | loop fusion | flops 262144 | bytes 1052672
  101.3 4.4 %select_dynamic-update-slice_fusion.19 = (bf16[6,4,128,128]{3,2,1,0:T(8,128)(2,1)S(1)}, bf16[6,4,128,128]{3,2,1,0:T(8,128)(2,1)}, bf16[6,4,128,128]{3,2,1,0:T(8,128)(2,1)}, bf16[6,4,128,128]{3,2,1,0:T(8,128)(2,1)}) fusion(bf16[6,4,128,128]{3,2,1,0:T(8,128)(2,1)S(1)} %get-tuple-element.23, bf16[64,4,128,128]{3,2,1,0:T(8,128)(2,1)} %all-gather.2.cloned.1.call-done, ...), kind=kLoop, calls=%fused_computation.93 | loop fusion | flops 262144 | bytes 1052672
  105.7 4.5 %select_dynamic-update-slice_fusion.18 = (bf16[6,4,128,128]{3,2,1,0:T(8,128)(2,1)S(1)}, bf16[6,4,128,128]{3,2,1,0:T(8,128)(2,1)}, bf16[6,4,128,128]{3,2,1,0:T(8,128)(2,1)}, bf16[6,4,128,128]{3,2,1,0:T(8,128)(2,1)}) fusion(bf16[6,4,128,128]{3,2,1,0:T(8,128)(2,1)S(1)} %get-tuple-element.19, bf16[64,4,128,128]{3,2,1,0:T(8,128)(2,1)} %all-gather.2.cloned.1.call-done, ...), kind=kLoop, calls=%fused_computation.92 | loop fusion | flops 262144 | bytes 1052672 | tf_op jit(solution)/shard_map/stack | solution.py:76
  110.2 1.1 collective-permute-start.3
  111.3 2.5 %collective-permute-start.5 = (bf16[6,4,128,128]{3,2,1,0:T(8,128)(2,1)}, bf16[6,4,128,128]{3,2,1,0:T(8,128)(2,1)}, u32[]{:S(2)}, u32[]{:S(2)}) collective-permute-start(bf16[6,4,128,128]{3,2,1,0:T(8,128)(2,1)} %get-tuple-element.17), channel_id=1, source_target_pairs={{0,64},{32,96},{64,0},{96,32},{1,65},{33,97},{65,1},{97,33},{2,66}... | collective-permute-start | bytes 2359304 | tf_op jit(solution)/shard_map/ppermute | solution.py:84
  113.8 1.2 collective-permute-start.7
  115.0 1.0 multiply_reduce_fusion
  116.7 4.8 %fusion.104 = (f32[4,512]{1,0:T(4,128)S(1)}, f32[4,512,512]{1,2,0:T(8,128)}) fusion(pred[512,512]{0,1:T(8,128)(4,1)S(1)} %fusion.42, bf16[512,4,128]{0,2,1:T(8,128)(2,1)S(1)} %add_convert_fusion.1, bf16[512,4,128]{0,2,1:T(8,128)(2,1)} %bitcast.181), kind=kOutput, calls=%fused_computation.176 | convolution fusion | flops 272630272 | bytes 5513216 | tf_op jit(solution)/shard_map/sub | solution.py:144
  121.5 8.7 %collective-permute-done.3 = bf16[6,4,128,128]{3,2,1,0:T(8,128)(2,1)} collective-permute-done((bf16[6,4,128,128]{3,2,1,0:T(8,128)(2,1)}, bf16[6,4,128,128]{3,2,1,0:T(8,128)(2,1)}, u32[]{:S(2)}, u32[]{:S(2)}) %collective-permute-start.3) | collective-permute-done | bytes 786464 | tf_op jit(solution)/shard_map/ppermute | solution.py:84
  130.1 17.8 %collective-permute-done.5 = bf16[6,4,128,128]{3,2,1,0:T(8,128)(2,1)} collective-permute-done((bf16[6,4,128,128]{3,2,1,0:T(8,128)(2,1)}, bf16[6,4,128,128]{3,2,1,0:T(8,128)(2,1)}, u32[]{:S(2)}, u32[]{:S(2)}) %collective-permute-start.5) | collective-permute-done | bytes 786464 | tf_op jit(solution)/shard_map/ppermute | solution.py:84
  148.0 3.7 %fusion.1 = f32[512,4,128]{0,2,1:T(8,128)} fusion(f32[512,6]{0,1:T(8,128)S(1)} %fusion.59, bf16[512,4,128]{0,2,1:T(8,128)(2,1)S(1)} %add_convert_fusion.1, bf16[6,4,128,128]{3,2,1,0:T(8,128)(2,1)} %collective-permute-done.7, bf16[6,4,128,128]{3,2,1,0:T(8,128)(2,1)} %collective-permute-done.5, bf16[6,4,128,128]{3,2,1,0:T(8,128)(2,1)} %collective-permute-done.3, ...), kind=kOutput, calls=%fused_computation.2 | convolution fusion | flops 408682496 | bytes 4730880 | tf_op jit(solution)/shard_map/thi,shij->tshj/dot_general | solution.py:137
  151.7 4.1 %multiply_reduce_fusion.1 = (f32[512,4]{0,1:T(4,128)S(1)}, f32[512,4,128]{0,2,1:T(8,128)}) fusion(f32[512,4,128]{0,2,1:T(8,128)} %fusion.1, f32[512,4]{0,1:T(4,128)S(1)} %copy-done.21, bf16[512,4,128]{0,2,1:T(8,128)(2,1)S(1)} %bitcast.179, f32[4,512]{1,0:T(4,128)S(1)} %bitcast.188, pred[512,512]{0,1:T(8,128)(4,1)S(1)} %fusion.42, ...), kind=kOutput, calls=%fused_computation.59 | convolution fusion | flops 543160320 | bytes 3956736 | tf_op jit(solution)/shard_map/hqk,khd->qhd/dot_general | solution.py:149
  155.8 3.4 %fusion.29 = bf16[512,4,128]{0,2,1:T(8,128)(2,1)S(1)} fusion(bf16[512,4,128]{0,2,1:T(8,128)(2,1)S(1)} %bitcast.180, f32[4,512,512]{1,2,0:T(8,128)} %get-tuple-element.96, f32[4,512]{1,0:T(4,128)S(1)} %get-tuple-element.95, f32[512,4]{0,1:T(4,128)S(1)} %add_rsqrt_fusion, f32[512,4]{0,1:T(4,128)S(1)} %copy-done.24, f32[512,4,128]{0,2,1:T(8,128)} %get-tuple-element.98, ...), kind=kOutput, calls=%fused_computation.42 | convolution fusion | flops 272105472 | bytes 7372800 | tf_op jit(solution)/shard_map/hqk,khd->qhd/dot_general | solution.py:146
  159.3 0.7 fusion.107
  160.0 1.1 constant_dynamic-slice_fusion
  161.1 1.5 collective-permute-start.8
  162.7 2.6 %collective-permute-done.8 = f32[256,1024]{1,0:T(8,128)} collective-permute-done((f32[256,1024]{1,0:T(8,128)}, f32[256,1024]{1,0:T(8,128)}, u32[]{:S(2)}, u32[]{:S(2)}) %collective-permute-start.8) | collective-permute-done | bytes 1048608 | tf_op jit(solution)/shard_map/ppermute | solution.py:21
  165.3 1.5 fusion.36
  166.8 4.4 %fusion.6 = f32[2,256,1408]{2,1,0:T(8,128)S(1)} fusion(bf16[3,1024,1408]{2,1,0:T(8,128)(2,1)} %param.25, bf16[256,1024]{1,0:T(8,128)(2,1)S(1)} %get-tuple-element.6, f32[1024]{0:T(1024)S(1)} %bitcast.192, f32[256]{0:T(256)S(1)} %add_rsqrt_fusion.1), kind=kOutput, calls=%fused_computation.12 | convolution fusion | flops 1477443584 | bytes 9180160 | tf_op jit(solution)/shard_map/td,kdf->ktf/dot_general | solution.py:163
  171.2 2.9 %fusion.14 = f32[256,1024]{1,0:T(8,128)S(1)} fusion(bf16[3,1024,1408]{2,1,0:T(8,128)(2,1)} %param.25, f32[2,256,1408]{2,1,0:T(8,128)S(1)} %fusion.6), kind=kOutput, calls=%fused_computation.17 | convolution fusion | flops 740360192 | bytes 6815744 | tf_op jit(solution)/shard_map/tf,df->td/dot_general | solution.py:167
  174.1 4.4 %fusion.9 = f32[2,256,1408]{2,1,0:T(8,128)S(1)} fusion(bf16[3,1024,1408]{2,1,0:T(8,128)(2,1)} %collective-permute-done.9, bf16[256,1024]{1,0:T(8,128)(2,1)S(1)} %get-tuple-element.6, f32[1024]{0:T(1024)S(1)} %bitcast.193, f32[256]{0:T(256)S(1)} %add_rsqrt_fusion.1), kind=kOutput, calls=%fused_computation.13 | convolution fusion | flops 1477443584 | bytes 9180160 | tf_op jit(solution)/shard_map/td,kdf->ktf/dot_general | solution.py:163
  178.5 3.8 %fusion.30 = bf16[256,1024]{1,0:T(8,128)(2,1)} fusion(f32[256,1024]{1,0:T(8,128)S(1)} %fusion.14, bf16[3,1024,1408]{2,1,0:T(8,128)(2,1)} %collective-permute-done.9, bf16[256,1024]{1,0:T(8,128)(2,1)S(1)} %get-tuple-element.6, f32[2,256,1408]{2,1,0:T(8,128)S(1)} %fusion.9), kind=kOutput, calls=%fused_computation.43 | convolution fusion | flops 741408768 | bytes 7864320 | tf_op jit(solution)/shard_map/tf,df->td/dot_general | solution.py:167
  (95 shorter events, 4.1 us)
Async XLA Ops:
  6.5 58.1 %copy-start = (bf16[3,1024,512]{2,1,0:T(8,128)(2,1)S(1)}, bf16[3,1024,512]{2,1,0:T(8,128)(2,1)}, u32[]{:S(2)}) copy-start(bf16[3,1024,512]{2,1,0:T(8,128)(2,1)} %param.15) | copy-start | bytes 9437188
  6.5 15.0 %copy-start.30 = (s32[1,6]{1,0:T(1,128)S(1)}, s32[1,6]{1,0:T(1,128)}, u32[]{:S(2)}) copy-start(s32[1,6]{1,0:T(1,128)} %param.22) | copy-start | bytes 76
  6.5 11.6 %copy-start.22 = (f32[2,1024]{1,0:T(2,128)S(1)}, f32[2,1024]{1,0:T(2,128)}, u32[]{:S(2)}) copy-start(f32[2,1024]{1,0:T(2,128)} %param.14) | copy-start | bytes 24580
  6.5 14.8 %copy-start.31 = (s32[1,2,3]{2,1,0:T(2,128)S(1)}, s32[1,2,3]{2,1,0:T(2,128)}, u32[]{:S(2)}) copy-start(s32[1,2,3]{2,1,0:T(2,128)} %param.20) | copy-start | bytes 76
  6.5 76.9 %all-gather.2.cloned.1.call-start = ((), (), s32[]{:S(2)}) async-start(), calls=%async_computation | async-start | bytes 8912896 | tf_op jit(solution)/shard_map/all_gather | solution.py:58
  7.3 27.0 %collective-permute-start.2 = (s32[6]{0:T(128)}, s32[6]{0:T(128)}, u32[]{:S(2)}, u32[]{:S(2)}) collective-permute-start(s32[6]{0:T(128)} %bitcast.196), channel_id=1, source_target_pairs={{0,96},{32,0},{64,32},{96,64},{1,97},{33,1},{65,33},{97,65},{2,98}... | collective-permute-start | bytes 80 | tf_op jit(solution)/shard_map/ppermute | solution.py:65
  11.9 24.7 %collective-permute-start.4 = (s32[6]{0:T(128)}, s32[6]{0:T(128)}, u32[]{:S(2)}, u32[]{:S(2)}) collective-permute-start(s32[6]{0:T(128)} %bitcast.197), channel_id=1, source_target_pairs={{0,64},{32,96},{64,0},{96,32},{1,65},{33,97},{65,1},{97,33},{2,66}... | collective-permute-start | bytes 80 | tf_op jit(solution)/shard_map/ppermute | solution.py:65
  11.9 25.4 %collective-permute-start.6 = (s32[6]{0:T(128)}, s32[6]{0:T(128)}, u32[]{:S(2)}, u32[]{:S(2)}) collective-permute-start(s32[6]{0:T(128)} %bitcast.198), channel_id=1, source_target_pairs={{0,32},{32,64},{64,96},{96,0},{1,33},{33,65},{65,97},{97,1},{2,34}... | collective-permute-start | bytes 80 | tf_op jit(solution)/shard_map/ppermute | solution.py:65
  15.4 55.7 %collective-permute-start.1 = (bf16[32,1024,16]{1,0,2:T(8,128)(2,1)}, bf16[32,1024,16]{1,0,2:T(8,128)(2,1)}, u32[]{:S(2)}, u32[]{:S(2)}) collective-permute-start(bf16[32,1024,16]{1,0,2:T(8,128)(2,1)} %copy.49), channel_id=1, source_target_pairs={{0,1},{1,0},{2,3},{3,2},{4,5},{5,4},{6,7},{7,6},{8,9},{9,8},{10,11... | collective-permute-start | bytes 3145736 | tf_op jit(solution)/shard_map/ppermute | solution.py:21
  18.2 3.2 %copy-start.19 = (f32[256]{0:T(256)}, f32[256]{0:T(256)S(1)}, u32[]{:S(2)}) copy-start(f32[256]{0:T(256)S(1)} %add_rsqrt_fusion.2) | copy-start | bytes 3076
  18.8 0.6 copy-start.13
  21.4 30.7 %collective-permute-start = (bf16[256,1024]{1,0:T(8,128)(2,1)}, bf16[256,1024]{1,0:T(8,128)(2,1)}, u32[]{:S(2)}, u32[]{:S(2)}) collective-permute-start(bf16[256,1024]{1,0:T(8,128)(2,1)} %fusion.34), channel_id=1, source_target_pairs={{0,1},{1,0},{2,3},{3,2},{4,5},{5,4},{6,7},{7,6},{8,9},{9,8},{10,11... | collective-permute-start | bytes 1572872 | tf_op jit(solution)/shard_map/ppermute | solution.py:21
  26.3 25.8 %copy-start.2 = (bf16[256,1024]{1,0:T(8,128)(2,1)S(1)}, bf16[256,1024]{1,0:T(8,128)(2,1)}, u32[]{:S(2)}) copy-start(bf16[256,1024]{1,0:T(8,128)(2,1)} %param.13) | copy-start | bytes 1572868
  26.3 25.8 %copy-start.14 = (f32[1,1024]{1,0:T(1,128)S(1)}, f32[1,1024]{1,0:T(1,128)}, u32[]{:S(2)}) copy-start(f32[1,1024]{1,0:T(1,128)} %copy-done.13) | copy-start | bytes 12292
  26.3 25.8 %copy-start.20 = (f32[256]{0:T(256)S(1)}, f32[256]{0:T(256)}, u32[]{:S(2)}) copy-start(f32[256]{0:T(256)} %copy-done.19) | copy-start | bytes 3076
  28.5 27.4 %copy-start.27 = (f32[4]{0:T(128)S(1)}, f32[4]{0:T(128)}, u32[]{:S(2)}) copy-start(f32[4]{0:T(128)} %param.17) | copy-start | bytes 52
  34.3 139.8 %collective-permute-start.9 = (bf16[3,1024,1408]{2,1,0:T(8,128)(2,1)}, bf16[3,1024,1408]{2,1,0:T(8,128)(2,1)}, u32[]{:S(2)}, u32[]{:S(2)}) collective-permute-start(bf16[3,1024,1408]{2,1,0:T(8,128)(2,1)} %param.25), channel_id=1, source_target_pairs={{0,1},{1,0},{2,3},{3,2},{4,5},{5,4},{6,7},{7,6},{8,9},{9,8},{10,11... | collective-permute-start | bytes 25952264 | tf_op jit(solution)/shard_map/ppermute | solution.py:21
  53.4 0.8 copy-start.8
  53.4 1.9 copy-start.10
  55.3 0.6 copy-start.15
  64.7 3.1 %copy-start.16 = (f32[2,512,4]{1,2,0:T(4,128)S(1)}, f32[2,512,4]{1,2,0:T(4,128)}, u32[]{:S(2)}) copy-start(f32[2,512,4]{1,2,0:T(4,128)} %copy-done.15) | copy-start | bytes 49156
  64.7 3.2 %copy-start.28 = (f32[4]{0:T(128)S(1)}, f32[4]{0:T(128)}, u32[]{:S(2)}) copy-start(f32[4]{0:T(128)} %param.17) | copy-start | bytes 52
  64.7 4.0 %copy-start.12 = (f32[6,512]{1,0:T(8,128)S(1)}, f32[6,512]{1,0:T(8,128)}, u32[]{:S(2)}) copy-start(f32[6,512]{1,0:T(8,128)} %fusion.60) | copy-start | bytes 36868
  67.8 3.3 %copy-start.4 = (f32[6,1024,16]{1,0,2:T(8,128)S(1)}, f32[6,1024,16]{1,0,2:T(8,128)}, u32[]{:S(2)}) copy-start(f32[6,1024,16]{1,0,2:T(8,128)} %fusion.72) | copy-start | bytes 1179652
  67.8 3.3 %copy-start.25 = (s32[1,6]{1,0:T(1,128)S(1)}, s32[1,6]{1,0:T(1,128)}, u32[]{:S(2)}) copy-start(s32[1,6]{1,0:T(1,128)} %param.21) | copy-start | bytes 76
  67.9 3.2 %copy-start.29 = (s32[32]{0:T(128)S(1)}, s32[32]{0:T(128)}, u32[]{:S(2)}) copy-start(s32[32]{0:T(128)} %iota_add_fusion) | copy-start | bytes 388
  68.6 4.2 %copy-start.9 = (bf16[256,1024]{1,0:T(8,128)(2,1)S(1)}, bf16[256,1024]{1,0:T(8,128)(2,1)}, u32[]{:S(2)}) copy-start(bf16[256,1024]{1,0:T(8,128)(2,1)} %copy-done.8) | copy-start | bytes 1572868
  68.6 4.2 %copy-start.11 = (bf16[256,1024]{1,0:T(8,128)(2,1)S(1)}, bf16[256,1024]{1,0:T(8,128)(2,1)}, u32[]{:S(2)}) copy-start(bf16[256,1024]{1,0:T(8,128)(2,1)} %copy-done.10) | copy-start | bytes 1572868
  110.2 4.8 %copy-start.17 = (bf16[6,4,128,128]{3,2,1,0:T(8,128)(2,1)}, bf16[6,4,128,128]{3,2,1,0:T(8,128)(2,1)S(1)}, u32[]{:S(2)}) copy-start(bf16[6,4,128,128]{3,2,1,0:T(8,128)(2,1)S(1)} %get-tuple-element.15) | copy-start | bytes 2359300
  110.2 19.9 %collective-permute-start.3 = (bf16[6,4,128,128]{3,2,1,0:T(8,128)(2,1)}, bf16[6,4,128,128]{3,2,1,0:T(8,128)(2,1)}, u32[]{:S(2)}, u32[]{:S(2)}) collective-permute-start(bf16[6,4,128,128]{3,2,1,0:T(8,128)(2,1)} %get-tuple-element.18), channel_id=1, source_target_pairs={{0,32},{32,64},{64,96},{96,0},{1,33},{33,65},{65,97},{97,1},{2,34}... | collective-permute-start | bytes 2359304 | tf_op jit(solution)/shard_map/ppermute | solution.py:84
  111.3 36.6 %collective-permute-start.5 = (bf16[6,4,128,128]{3,2,1,0:T(8,128)(2,1)}, bf16[6,4,128,128]{3,2,1,0:T(8,128)(2,1)}, u32[]{:S(2)}, u32[]{:S(2)}) collective-permute-start(bf16[6,4,128,128]{3,2,1,0:T(8,128)(2,1)} %get-tuple-element.17), channel_id=1, source_target_pairs={{0,64},{32,96},{64,0},{96,32},{1,65},{33,97},{65,1},{97,33},{2,66}... | collective-permute-start | bytes 2359304 | tf_op jit(solution)/shard_map/ppermute | solution.py:84
  113.8 34.1 %collective-permute-start.7 = (bf16[6,4,128,128]{3,2,1,0:T(8,128)(2,1)}, bf16[6,4,128,128]{3,2,1,0:T(8,128)(2,1)}, u32[]{:S(2)}, u32[]{:S(2)}) collective-permute-start(bf16[6,4,128,128]{3,2,1,0:T(8,128)(2,1)} %get-tuple-element.16), channel_id=1, source_target_pairs={{0,96},{32,0},{64,32},{96,64},{1,97},{33,1},{65,33},{97,65},{2,98}... | collective-permute-start | bytes 2359304 | tf_op jit(solution)/shard_map/ppermute | solution.py:84
  116.7 31.3 %copy-start.18 = (bf16[6,4,128,128]{3,2,1,0:T(8,128)(2,1)S(1)}, bf16[6,4,128,128]{3,2,1,0:T(8,128)(2,1)}, u32[]{:S(2)}) copy-start(bf16[6,4,128,128]{3,2,1,0:T(8,128)(2,1)} %copy-done.17) | copy-start | bytes 2359300
  147.9 3.8 %copy-start.6 = (bf16[1,512,512]{1,2,0:T(8,128)(2,1)S(1)}, bf16[1,512,512]{1,2,0:T(8,128)(2,1)}, u32[]{:S(2)}) copy-start(bf16[1,512,512]{1,2,0:T(8,128)(2,1)} %get-tuple-element.40) | copy-start | bytes 1572868
  147.9 3.8 %copy-start.7 = (bf16[1,512,512]{1,2,0:T(8,128)(2,1)S(1)}, bf16[1,512,512]{1,2,0:T(8,128)(2,1)}, u32[]{:S(2)}) copy-start(bf16[1,512,512]{1,2,0:T(8,128)(2,1)} %get-tuple-element.39) | copy-start | bytes 1572868
  147.9 3.8 %copy-start.21 = (f32[512,4]{0,1:T(4,128)S(1)}, f32[512,4]{0,1:T(4,128)}, u32[]{:S(2)}) copy-start(f32[512,4]{0,1:T(4,128)} %fusion.68) | copy-start | bytes 24580
  147.9 3.8 %copy-start.23 = (f32[1,4,4,128]{3,1,2,0:T(4,128)S(1)}, f32[1,4,4,128]{3,1,2,0:T(4,128)}, u32[]{:S(2)}) copy-start(f32[1,4,4,128]{3,1,2,0:T(4,128)} %copy.85) | copy-start | bytes 24580
  151.7 4.1 %copy-start.24 = (f32[512,4]{0,1:T(4,128)S(1)}, f32[512,4]{0,1:T(4,128)}, u32[]{:S(2)}) copy-start(f32[512,4]{0,1:T(4,128)} %fusion.67) | copy-start | bytes 24580
  155.8 3.5 %copy-start.5 = (bf16[512,1024]{1,0:T(8,128)(2,1)S(1)}, bf16[512,1024]{1,0:T(8,128)(2,1)}, u32[]{:S(2)}) copy-start(bf16[512,1024]{1,0:T(8,128)(2,1)} %param.24) | copy-start | bytes 3145732
  159.3 6.0 %copy-start.3 = (bf16[256,1024]{1,0:T(8,128)(2,1)S(1)}, bf16[256,1024]{1,0:T(8,128)(2,1)}, u32[]{:S(2)}) copy-start(bf16[256,1024]{1,0:T(8,128)(2,1)} %param.13) | copy-start | bytes 1572868
  160.0 6.8 %copy-start.26 = (f32[1,1024]{1,0:T(1,128)S(1)}, f32[1,1024]{1,0:T(1,128)}, u32[]{:S(2)}) copy-start(f32[1,1024]{1,0:T(1,128)} %get-tuple-element.43) | copy-start | bytes 12292
  161.1 4.2 %collective-permute-start.8 = (f32[256,1024]{1,0:T(8,128)}, f32[256,1024]{1,0:T(8,128)}, u32[]{:S(2)}, u32[]{:S(2)}) collective-permute-start(f32[256,1024]{1,0:T(8,128)} %constant_dynamic-slice_fusion), channel_id=1, source_target_pairs={{0,1},{1,0},{2,3},{3,2},{4,5},{5,4},{6,7},{7,6},{8,9},{9,8},{10,11... | collective-permute-start | bytes 3145736 | tf_op jit(solution)/shard_map/ppermute | solution.py:21
  178.5 3.9 %copy-start.1 = (bf16[3,1024,512]{2,1,0:T(8,128)(2,1)S(1)}, bf16[3,1024,512]{2,1,0:T(8,128)(2,1)}, u32[]{:S(2)}) copy-start(bf16[3,1024,512]{2,1,0:T(8,128)(2,1)} %param.15) | copy-start | bytes 9437188
Sparse Core Ops, SparseCore 0:
  9.5 73.8 all-gather.1

commit v3 on v1

--- a/solution.py
+++ b/solution.py
@@ -55,14 +55,34 @@
     ff_other = swap(feedforward_weight)
     down_other = swap(adapter_down_factor)
 
-    plane = lax.all_gather(caches, ("y", "x"), axis=0, tiled=True)
-    per_plane = plane.shape[0]
-    line_index = lax.all_gather(request_cache_index[0], "z", axis=0)
-    local = line_index - lax.axis_index("z") * per_plane
-    valid = (local >= 0) & (local < per_plane)
-    picked = plane[jnp.clip(local, 0, per_plane - 1)]
-    slots = jnp.where(valid[:, :, None, None, None], picked, jnp.zeros_like(picked))
-    states = lax.psum_scatter(slots, "z", scatter_dimension=0, tiled=True)[0]
+    z_count = lax.axis_size("z")
+    z_here = lax.axis_index("z")
+    own_index = request_cache_index[0]
+    shifts = range(1, z_count)
+
+    def along_z(value, d):
+        return lax.ppermute(value, "z", perm=[(i, (i + d) % z_count) for i in range(z_count)])
+
+    shifted = {d: along_z(own_index, d) for d in shifts}
+    line_rows = jnp.stack([own_index] + [shifted[z_count - d] for d in shifts])
+    per_plane = caches.shape[0] * lax.axis_size("y") * lax.axis_size("x")
+    local = line_rows - z_here * per_plane
+    onehot = (local[:, :, None] == jnp.arange(per_plane, dtype=jnp.int32)[None, None, :]).astype(
+        jnp.bfloat16
+    )
+    chunk_count = 2
+    chunk = caches.shape[1] // chunk_count
+    state_parts = []
+    for c in range(chunk_count):
+        plane = lax.all_gather(caches[:, c * chunk:(c + 1) * chunk], ("y", "x"), axis=0, tiled=True)
+        picked = jnp.einsum(
+            "dsn,nhij->dshij", onehot, plane, preferred_element_type=jnp.float32
+        ).astype(jnp.bfloat16)
+        total = picked[0].astype(jnp.float32)
+        for d in shifts:
+            total = total + along_z(picked[d], d).astype(jnp.float32)
+        state_parts.append(total.astype(jnp.bfloat16))
+    states = jnp.concatenate(state_parts, axis=1)
 
     normalized_rows = rms_scale(tokens, norm_gain_pair[0])
     gathered = pair_rows(normalized_rows, swap(normalized_rows), col)

time: 178 us -> 193 us (1.084)
  starting transfers between devices: 1.23 us -> 18.8 us
  blocking collectives: 10.1 us -> 0 us
  matrix products: 42.3 us -> 50.6 us
  local copies, waits for them, and re-layouts: 22.9 us -> 18.3 us
    ppermute x0 -> x9, waiting for transfers between devices: none -> 16.2 us  [along_z(): lax.ppermute(value, 'z', perm=[(i, (i + d) % z_count) for i in range(z_co...]
    ppermute x0 -> x9, starting transfers between devices: none -> 15.2 us  [along_z(): lax.ppermute(value, 'z', perm=[(i, (i + d) % z_count) for i in range(z_co...]
    all_gather x1 -> x2, waiting for transfers between devices: 63.2 us -> 49.4 us  [on_device(): lax.all_gather(caches[:, c * chunk:(c + 1) * chunk], ('y', 'x'), axis=0,...]
    gather x2 -> x0, local copies, waits for them, and re-layouts: 10.9 us -> none  [on_device(): picked = plane[jnp.clip(local, 0, per_plane - 1)]]
    all_gather x1 -> x0, blocking collectives: 10.1 us -> none  [on_device(): line_index = lax.all_gather(request_cache_index[0], 'z', axis=0)]
    dot_general x0 -> x2, matrix products: none -> 9.65 us  [on_device(): jnp.einsum('dsn,nhij->dshij', onehot, plane, preferred_element_type=jnp.f...]
    select_n x2 -> x0, other arithmetic: 3.81 us -> none  [the longest x1 3.81 us: on_device(): jnp.where(valid[:, :, None, None, None], picked, jnp.zeros_like(picked))]
    convert_element_type x0 -> x2, other arithmetic: none -> 3.32 us  [on_device(): state_parts.append(total.astype(jnp.bfloat16))]
  transfers between devices with their start and end apart: 6 -> 15, of which waited for: 2 -> 5; matrix products, arithmetic and copies ran while one was open for 34% -> 40% of each run, Pallas kernels for 0% -> 0%
where the time goes in v3:
time: 193 us; the launch traced here: 192 us
  waiting for transfers between devices  68.9 us (36%)
  matrix products  50.6 us (26%)
  other arithmetic  21.1 us (11%)
  starting transfers between devices  18.8 us (10%)
  local copies, waits for them, and re-layouts  18.3 us (9%)
  between operations  13.9 us (7%)
    all_gather x2, waiting for transfers between devices, on_device(): lax.all_gather(caches[:, c * chunk:(c + 1) * chunk], ('y', 'x'), axis=0,...  49.4 us
    ppermute x9, waiting for transfers between devices, along_z(): lax.ppermute(value, 'z', perm=[(i, (i + d) % z_count) for i in range(z_co...  16.2 us
    ppermute x9, starting transfers between devices, along_z(): lax.ppermute(value, 'z', perm=[(i, (i + d) % z_count) for i in range(z_co...  15.2 us
    dot_general x2, matrix products, on_device(): jnp.einsum('dsn,nhij->dshij', onehot, plane, preferred_element_type=jnp.f...  9.65 us
    dot_general x2, matrix products, feed_half(): jnp.einsum('td,kdf->ktf', normed_two, weight[:2], preferred_element_type=...  8.73 us
    unnamed x64, local copies, waits for them, and re-layouts  6.76 us
    dot_general x2, matrix products, feed_half(): jnp.einsum('tf,df->td', hidden, weight[2], preferred_element_type=jnp.flo...  6.71 us
    sub x1, matrix products, on_device(): weights = jnp.exp(masked - peak)  4.7 us
  transfers between devices with their start and end apart: 15, of which 5 were waited for; matrix products, arithmetic and copies ran while one was open for 40% of the time, Pallas kernels for 0%

profile of v3, /device:TPU:1, one launch (start us, length us, event | category | flops | bytes accessed | tf_op | source)
XLA Modules:
  0.0 191.7 jit_solution(15833018750686965384)
XLA Ops:
  6.5 2.1 %fusion.118 = (bf16[4,2,128,128]{3,2,1,0:T(8,128)(2,1)}, bf16[4,2,128,128]{3,2,1,0:T(8,128)(2,1)}) fusion(bf16[4,4,128,128]{3,2,1,0:T(8,128)(2,1)} %param.23), kind=kLoop, calls=%fused_computation.163 | loop fusion | bytes 1048576 | tf_op jit(solution)/shard_map/slice | solution.py:77
  8.7 0.7 all-gather.3.cloned.1.call-update
  9.4 2.5 %collective-permute-start.4 = (s32[6]{0:T(128)}, s32[6]{0:T(128)}, u32[]{:S(2)}, u32[]{:S(2)}) collective-permute-start(s32[6]{0:T(128)} %bitcast.189), channel_id=1, source_target_pairs={{0,32},{32,64},{64,96},{96,0},{1,33},{33,65},{65,97},{97,1},{2,34}... | collective-permute-start | bytes 80 | tf_op jit(solution)/shard_map/ppermute | solution.py:64
  11.9 3.3 %collective-permute-start.3 = (s32[6]{0:T(128)}, s32[6]{0:T(128)}, u32[]{:S(2)}, u32[]{:S(2)}) collective-permute-start(s32[6]{0:T(128)} %bitcast.190), channel_id=1, source_target_pairs={{0,64},{32,96},{64,0},{96,32},{1,65},{33,97},{65,1},{97,33},{2,66}... | collective-permute-start | bytes 80 | tf_op jit(solution)/shard_map/ppermute | solution.py:64
  15.2 0.7 collective-permute-start.2
  15.9 1.2 fusion.45
  17.2 1.4 fusion.119
  18.6 0.6 copy-done.16
  19.1 2.0 %fusion.47 = bf16[256,1024]{1,0:T(8,128)(2,1)} fusion(bf16[256,1024]{1,0:T(8,128)(2,1)} %param.13, f32[1024]{0:T(1024)S(1)} %bitcast.178, f32[256]{0:T(256)S(1)} %add_rsqrt_fusion.2), kind=kLoop, calls=%fused_computation.58 | loop fusion | flops 1048576 | bytes 1053696 | tf_op jit(solution)/shard_map/convert_element_type | solution.py:17
  21.2 1.5 collective-permute-start
  22.7 2.8 %copy.55 = bf16[32,1024,16]{1,0,2:T(8,128)(2,1)} copy(bf16[32,1024,16]{1,2,0:T(8,128)(2,1)} %param.18) | data formatting | bytes 2097152 | tf_op args[5]
  25.9 0.7 fusion.82
  26.9 2.5 %convolution_convert_fusion = bf16[6,16,512]{2,0,1:T(8,128)(2,1)S(1)} fusion(bf16[64,16,512]{2,1,0:T(8,128)(2,1)} %param.19, s32[6]{0:T(128)} %bitcast.182), kind=kOutput, calls=%fused_computation.54 | convolution fusion | flops 6340992 | bytes 1146904 | tf_op jit(solution)/shard_map/gq,qjl->gjl/dot_general | solution.py:116
  29.4 0.5 iota_add_fusion.1
  29.9 0.5 iota_add_fusion
  30.4 3.3 %fusion.96 = f32[6,1024,16]{1,0,2:T(8,128)} fusion(s32[32]{0:T(128)} %iota_add_fusion.1, s32[6]{0:T(128)} %bitcast.183, bf16[32,1024,16]{1,2,0:T(8,128)(2,1)} %param.18), kind=kOutput, calls=%fused_computation.135 | convolution fusion | flops 6291648 | bytes 1441944 | tf_op jit(solution)/shard_map/sa,adr->sdr/dot_general | solution.py:106
  33.7 0.5 collective-permute-start.12
  34.2 1.3 add_subtract_fusion
  35.4 1.5 broadcast_select_fusion.1
  37.0 0.8 copy-done.11
  38.2 0.6 copy-done.17
  38.8 0.7 fusion.114
  39.4 1.3 reshape.312
  40.7 3.1 %reduce-window.18 = f32[4,4,128]{2,1,0:T(4,128)} reduce-window(f32[4,4,128]{2,1,0:T(4,128)} %reshape.312, f32[]{:T(128)} %constant.18.clone.1), window={size=1x1x128 pad=0_0x0_0x127_0}, to_apply=%region_7.8 | reduce-window | flops 260096 | bytes 16388 | tf_op jit(solution)/shard_map/reduce-window.1
  43.8 1.4 slice_reduce_fusion
  45.3 1.4 reduce-window.19
  46.7 0.8 add_bitcast_fusion
  47.5 3.1 %fusion.120 = (bf16[3,512,512]{1,2,0:T(8,128)(2,1)S(1)}, f32[3,512,512]{1,2,0:T(8,128)S(1)}) fusion(bf16[3,1024,512]{2,1,0:T(8,128)(2,1)S(1)} %copy-done, bf16[256,1024]{1,0:T(8,128)(2,1)} %copy-done.13, bf16[256,1024]{1,0:T(8,128)(2,1)} %copy-done.11), kind=kOutput, calls=%fused_computation.165 | convolution fusion | flops 1613496320 | bytes 8912896 | tf_op jit(solution)/shard_map/td,kdc->ktc/dot_general | solution.py:96
  50.7 0.6 copy.104
  51.6 0.6 fusion.90
  52.2 0.6 fusion.89
  52.8 1.1 fusion.117
  53.9 1.5 fusion.44
  56.1 1.0 multiply_reduce_fusion
  57.7 6.6 %all-gather.5.cloned.1.call-done = bf16[64,2,128,128]{3,2,1,0:T(8,128)(2,1)} async-done(((bf16[4,2,128,128]{3,2,1,0:T(8,128)(2,1)}), bf16[64,2,128,128]{3,2,1,0:T(8,128)(2,1)}) %all-gather.5.cloned.1.call-update) | async-done | bytes 4194320 | tf_op jit(solution)/shard_map/all_gather | solution.py:77
  64.3 4.8 %fusion.32 = bf16[4,6,2,128,128]{4,1,3,2,0:T(8,128)(2,1)S(1)} fusion(bf16[64,2,128,128]{3,2,1,0:T(8,128)(2,1)} %all-gather.5.cloned.1.call-done, s32[4,6]{1,0:T(4,128)S(1)} %copy-done.27), kind=kOutput, calls=%fused_computation.33 | convolution fusion | flops 101451264 | bytes 5767264 | tf_op jit(solution)/shard_map/dsn,nhij->dshij/dot_general | solution.py:78
  69.1 1.3 slice_bitcast_fusion.10
  70.4 1.3 collective-permute-start.8
  71.6 1.4 collective-permute-start.10
  73.0 1.7 collective-permute-start.9
  74.7 42.8 %all-gather.3.cloned.1.call-done = bf16[64,2,128,128]{3,2,1,0:T(8,128)(2,1)} async-done(((bf16[4,2,128,128]{3,2,1,0:T(8,128)(2,1)}), bf16[64,2,128,128]{3,2,1,0:T(8,128)(2,1)}) %all-gather.3.cloned.1.call-update) | async-done | bytes 4194320 | tf_op jit(solution)/shard_map/all_gather | solution.py:77
  117.5 4.8 %fusion.29 = bf16[4,6,2,128,128]{4,1,3,2,0:T(8,128)(2,1)S(1)} fusion(bf16[64,2,128,128]{3,2,1,0:T(8,128)(2,1)} %all-gather.3.cloned.1.call-done, s32[4,6]{1,0:T(4,128)S(1)} %copy-done.27), kind=kOutput, calls=%fused_computation.32 | convolution fusion | flops 101451264 | bytes 5767264 | tf_op jit(solution)/shard_map/dsn,nhij->dshij/dot_general | solution.py:78
  122.4 1.3 copy-done.3
  123.7 1.2 slice_bitcast_fusion.14
  124.9 1.3 collective-permute-start.5
  126.2 1.4 collective-permute-start.7
  127.6 1.7 collective-permute-start.6
  129.3 4.7 %fusion.121 = (f32[4,512]{1,0:T(4,128)S(1)}, f32[4,512,512]{1,2,0:T(8,128)}) fusion(pred[512,512]{0,1:T(8,128)(4,1)S(1)} %fusion.61, bf16[512,4,128]{0,2,1:T(8,128)(2,1)S(1)} %add_convert_fusion, bf16[512,4,128]{0,2,1:T(8,128)(2,1)} %bitcast.174), kind=kOutput, calls=%fused_computation.166 | convolution fusion | flops 272630272 | bytes 5513216 | tf_op jit(solution)/shard_map/sub | solution.py:143
  134.0 1.5 fusion.54
  135.5 3.7 %collective-permute-done.5 = bf16[6,2,128,128]{3,0,2,1:T(8,128)(2,1)} collective-permute-done((bf16[6,2,128,128]{3,0,2,1:T(8,128)(2,1)}, bf16[6,2,128,128]{3,0,2,1:T(8,128)(2,1)}, u32[]{:S(2)}, u32[]{:S(2)}) %collective-permute-start.5) | collective-permute-done | bytes 393248 | tf_op jit(solution)/shard_map/ppermute | solution.py:64
  139.2 12.4 %collective-permute-done.6 = bf16[6,2,128,128]{3,0,2,1:T(8,128)(2,1)} collective-permute-done((bf16[6,2,128,128]{3,0,2,1:T(8,128)(2,1)}, bf16[6,2,128,128]{3,0,2,1:T(8,128)(2,1)}, u32[]{:S(2)}, u32[]{:S(2)}) %collective-permute-start.6) | collective-permute-done | bytes 393248 | tf_op jit(solution)/shard_map/ppermute | solution.py:64
  151.6 1.8 fusion.57
  153.7 2.0 %fusion.1 = f32[512,4,128]{0,2,1:T(8,128)} fusion(f32[512,6]{0,1:T(8,128)S(1)} %fusion.78, bf16[6,4,128,128]{3,0,2,1:T(8,128)(2,1)S(1)} %pad_maximum_fusion.1, bf16[512,4,128]{0,2,1:T(8,128)(2,1)S(1)} %copy-done.7), kind=kOutput, calls=%fused_computation.2 | convolution fusion | flops 405536768 | bytes 2371584 | tf_op jit(solution)/shard_map/thi,shij->tshj/dot_general | solution.py:136
  155.8 3.1 %multiply_reduce_fusion.1 = (f32[512,4]{0,1:T(4,128)S(1)}, f32[512,4,128]{0,2,1:T(8,128)S(1)}) fusion(f32[512,4,128]{0,2,1:T(8,128)} %fusion.1, f32[512,4]{0,1:T(4,128)S(1)} %copy-done.20, bf16[512,4,128]{0,2,1:T(8,128)(2,1)S(1)} %bitcast.172, f32[4,512]{1,0:T(4,128)S(1)} %bitcast.181, pred[512,512]{0,1:T(8,128)(4,1)S(1)} %fusion.61, ...), kind=kOutput, calls=%fused_computation.76 | convolution fusion | flops 543160320 | bytes 3956736 | tf_op jit(solution)/shard_map/hqk,khd->qhd/dot_general | solution.py:148
  158.9 2.8 %fusion.42 = bf16[512,4,128]{0,2,1:T(8,128)(2,1)S(1)} fusion(bf16[512,4,128]{0,2,1:T(8,128)(2,1)S(1)} %bitcast.173, f32[4,512,512]{1,2,0:T(8,128)} %get-tuple-element.24, f32[4,512]{1,0:T(4,128)S(1)} %get-tuple-element.23, f32[512,4,128]{0,2,1:T(8,128)S(1)} %get-tuple-element.26, f32[512,4]{0,1:T(4,128)S(1)} %add_rsqrt_fusion, f32[512,4]{0,1:T(4,128)S(1)} %copy-done.22), kind=kOutput, calls=%fused_computation.50 | convolution fusion | flops 271581184 | bytes 6316032 | tf_op jit(solution)/shard_map/hqk,khd->qhd/dot_general | solution.py:145
  161.7 0.7 fusion.124
  162.5 1.2 constant_dynamic-slice_fusion
  163.6 1.5 collective-permute-start.11
  165.2 2.6 %collective-permute-done.11 = f32[256,1024]{1,0:T(8,128)} collective-permute-done((f32[256,1024]{1,0:T(8,128)}, f32[256,1024]{1,0:T(8,128)}, u32[]{:S(2)}, u32[]{:S(2)}) %collective-permute-start.11) | collective-permute-done | bytes 1048608 | tf_op jit(solution)/shard_map/ppermute | solution.py:21
  167.8 1.5 fusion.49
  169.3 4.4 %fusion.12 = f32[2,256,1408]{2,1,0:T(8,128)S(1)} fusion(bf16[3,1024,1408]{2,1,0:T(8,128)(2,1)} %param.25, bf16[256,1024]{1,0:T(8,128)(2,1)S(1)} %get-tuple-element.6, f32[1024]{0:T(1024)S(1)} %bitcast.185, f32[256]{0:T(256)S(1)} %add_rsqrt_fusion.1), kind=kOutput, calls=%fused_computation.18 | convolution fusion | flops 1477443584 | bytes 9180160 | tf_op jit(solution)/shard_map/td,kdf->ktf/dot_general | solution.py:162
  173.7 2.9 %fusion.20 = f32[256,1024]{1,0:T(8,128)S(1)} fusion(bf16[3,1024,1408]{2,1,0:T(8,128)(2,1)} %param.25, f32[2,256,1408]{2,1,0:T(8,128)S(1)} %fusion.12), kind=kOutput, calls=%fused_computation.23 | convolution fusion | flops 740360192 | bytes 6815744 | tf_op jit(solution)/shard_map/tf,df->td/dot_general | solution.py:166
  176.6 4.4 %fusion.15 = f32[2,256,1408]{2,1,0:T(8,128)S(1)} fusion(bf16[3,1024,1408]{2,1,0:T(8,128)(2,1)} %collective-permute-done.12, bf16[256,1024]{1,0:T(8,128)(2,1)S(1)} %get-tuple-element.6, f32[1024]{0:T(1024)S(1)} %bitcast.186, f32[256]{0:T(256)S(1)} %add_rsqrt_fusion.1), kind=kOutput, calls=%fused_computation.19 | convolution fusion | flops 1477443584 | bytes 9180160 | tf_op jit(solution)/shard_map/td,kdf->ktf/dot_general | solution.py:162
  181.0 3.8 %fusion.43 = bf16[256,1024]{1,0:T(8,128)(2,1)} fusion(f32[256,1024]{1,0:T(8,128)S(1)} %fusion.20, bf16[3,1024,1408]{2,1,0:T(8,128)(2,1)} %collective-permute-done.12, bf16[256,1024]{1,0:T(8,128)(2,1)S(1)} %get-tuple-element.6, f32[2,256,1408]{2,1,0:T(8,128)S(1)} %fusion.15), kind=kOutput, calls=%fused_computation.51 | convolution fusion | flops 741408768 | bytes 7864320 | tf_op jit(solution)/shard_map/tf,df->td/dot_general | solution.py:166
  (93 shorter events, 3.1 us)
Async XLA Ops:
  6.5 40.9 %copy-start = (bf16[3,1024,512]{2,1,0:T(8,128)(2,1)S(1)}, bf16[3,1024,512]{2,1,0:T(8,128)(2,1)}, u32[]{:S(2)}) copy-start(bf16[3,1024,512]{2,1,0:T(8,128)(2,1)} %param.15) | copy-start | bytes 9437188
  6.5 19.0 %copy-start.30 = (s32[1,2,3]{2,1,0:T(2,128)S(1)}, s32[1,2,3]{2,1,0:T(2,128)}, u32[]{:S(2)}) copy-start(s32[1,2,3]{2,1,0:T(2,128)} %param.20) | copy-start | bytes 76
  6.5 57.7 %all-gather.5.cloned.1.call-start = ((), (), s32[]{:S(2)}) async-start(), calls=%async_computation.1 | async-start | bytes 4456448 | tf_op jit(solution)/shard_map/all_gather | solution.py:77
  8.6 108.9 %all-gather.3.cloned.1.call-start = ((), (), s32[]{:S(2)}) async-start(), calls=%async_computation | async-start | bytes 4456448 | tf_op jit(solution)/shard_map/all_gather | solution.py:77
  9.4 24.3 %collective-permute-start.4 = (s32[6]{0:T(128)}, s32[6]{0:T(128)}, u32[]{:S(2)}, u32[]{:S(2)}) collective-permute-start(s32[6]{0:T(128)} %bitcast.189), channel_id=1, source_target_pairs={{0,32},{32,64},{64,96},{96,0},{1,33},{33,65},{65,97},{97,1},{2,34}... | collective-permute-start | bytes 80 | tf_op jit(solution)/shard_map/ppermute | solution.py:64
  11.9 22.2 %collective-permute-start.3 = (s32[6]{0:T(128)}, s32[6]{0:T(128)}, u32[]{:S(2)}, u32[]{:S(2)}) collective-permute-start(s32[6]{0:T(128)} %bitcast.190), channel_id=1, source_target_pairs={{0,64},{32,96},{64,0},{96,32},{1,65},{33,97},{65,1},{97,33},{2,66}... | collective-permute-start | bytes 80 | tf_op jit(solution)/shard_map/ppermute | solution.py:64
  15.2 18.9 %collective-permute-start.2 = (s32[6]{0:T(128)}, s32[6]{0:T(128)}, u32[]{:S(2)}, u32[]{:S(2)}) collective-permute-start(s32[6]{0:T(128)} %bitcast.191), channel_id=1, source_target_pairs={{0,96},{32,0},{64,32},{96,64},{1,97},{33,1},{65,33},{97,65},{2,98}... | collective-permute-start | bytes 80 | tf_op jit(solution)/shard_map/ppermute | solution.py:64
  17.2 4.0 %copy-start.19 = (f32[256]{0:T(256)}, f32[256]{0:T(256)S(1)}, u32[]{:S(2)}) copy-start(f32[256]{0:T(256)S(1)} %add_rsqrt_fusion.2) | copy-start | bytes 3076
  18.6 0.6 copy-start.16
  21.2 14.3 %collective-permute-start = (bf16[256,1024]{1,0:T(8,128)(2,1)}, bf16[256,1024]{1,0:T(8,128)(2,1)}, u32[]{:S(2)}, u32[]{:S(2)}) collective-permute-start(bf16[256,1024]{1,0:T(8,128)(2,1)} %fusion.47), channel_id=1, source_target_pairs={{0,1},{1,0},{2,3},{3,2},{4,5},{5,4},{6,7},{7,6},{8,9},{9,8},{10,11... | collective-permute-start | bytes 1572872 | tf_op jit(solution)/shard_map/ppermute | solution.py:21
  25.5 28.4 %collective-permute-start.1 = (bf16[32,1024,16]{1,0,2:T(8,128)(2,1)}, bf16[32,1024,16]{1,0,2:T(8,128)(2,1)}, u32[]{:S(2)}, u32[]{:S(2)}) collective-permute-start(bf16[32,1024,16]{1,0,2:T(8,128)(2,1)} %copy.55), channel_id=1, source_target_pairs={{0,1},{1,0},{2,3},{3,2},{4,5},{5,4},{6,7},{7,6},{8,9},{9,8},{10,11... | collective-permute-start | bytes 3145736 | tf_op jit(solution)/shard_map/ppermute | solution.py:21
  29.9 7.9 %copy-start.29 = (bf16[2,1024,4]{1,2,0:T(4,128)(2,1)S(1)}, bf16[2,1024,4]{1,2,0:T(4,128)(2,1)}, u32[]{:S(2)}) copy-start(bf16[2,1024,4]{1,2,0:T(4,128)(2,1)} %param.16) | copy-start | bytes 49156
  29.9 8.9 %copy-start.25 = (f32[4]{0:T(128)S(1)}, f32[4]{0:T(128)}, u32[]{:S(2)}) copy-start(f32[4]{0:T(128)} %param.17) | copy-start | bytes 52
  33.7 142.9 %collective-permute-start.12 = (bf16[3,1024,1408]{2,1,0:T(8,128)(2,1)}, bf16[3,1024,1408]{2,1,0:T(8,128)(2,1)}, u32[]{:S(2)}, u32[]{:S(2)}) collective-permute-start(bf16[3,1024,1408]{2,1,0:T(8,128)(2,1)} %param.25), channel_id=1, source_target_pairs={{0,1},{1,0},{2,3},{3,2},{4,5},{5,4},{6,7},{7,6},{8,9},{9,8},{10,11... | collective-permute-start | bytes 25952264 | tf_op jit(solution)/shard_map/ppermute | solution.py:21
  37.0 0.8 copy-start.11
  37.0 1.2 copy-start.13
  38.1 0.6 copy-start.17
  47.5 3.1 %copy-start.18 = (f32[2,512,4]{1,2,0:T(4,128)S(1)}, f32[2,512,4]{1,2,0:T(4,128)}, u32[]{:S(2)}) copy-start(f32[2,512,4]{1,2,0:T(4,128)} %copy-done.17) | copy-start | bytes 49156
  47.5 3.1 %copy-start.26 = (f32[4]{0:T(128)S(1)}, f32[4]{0:T(128)}, u32[]{:S(2)}) copy-start(f32[4]{0:T(128)} %param.17) | copy-start | bytes 52
  47.5 3.9 %copy-start.15 = (f32[6,512]{1,0:T(8,128)S(1)}, f32[6,512]{1,0:T(8,128)}, u32[]{:S(2)}) copy-start(f32[6,512]{1,0:T(8,128)} %fusion.82) | copy-start | bytes 36868
  50.6 3.3 %copy-start.4 = (f32[6,1024,16]{1,0,2:T(8,128)S(1)}, f32[6,1024,16]{1,0,2:T(8,128)}, u32[]{:S(2)}) copy-start(f32[6,1024,16]{1,0,2:T(8,128)} %fusion.96) | copy-start | bytes 1179652
  50.6 3.3 %copy-start.23 = (s32[1,6]{1,0:T(1,128)S(1)}, s32[1,6]{1,0:T(1,128)}, u32[]{:S(2)}) copy-start(s32[1,6]{1,0:T(1,128)} %param.21) | copy-start | bytes 76
  50.6 3.3 %copy-start.28 = (s32[32]{0:T(128)S(1)}, s32[32]{0:T(128)}, u32[]{:S(2)}) copy-start(s32[32]{0:T(128)} %iota_add_fusion) | copy-start | bytes 388
  51.3 4.3 %copy-start.12 = (bf16[256,1024]{1,0:T(8,128)(2,1)S(1)}, bf16[256,1024]{1,0:T(8,128)(2,1)}, u32[]{:S(2)}) copy-start(bf16[256,1024]{1,0:T(8,128)(2,1)} %copy-done.11) | copy-start | bytes 1572868
  51.3 4.3 %copy-start.14 = (bf16[256,1024]{1,0:T(8,128)(2,1)S(1)}, bf16[256,1024]{1,0:T(8,128)(2,1)}, u32[]{:S(2)}) copy-start(bf16[256,1024]{1,0:T(8,128)(2,1)} %copy-done.13) | copy-start | bytes 1572868
  57.1 7.2 %copy-start.27 = (s32[4,6]{1,0:T(4,128)S(1)}, s32[4,6]{1,0:T(4,128)}, u32[]{:S(2)}) copy-start(s32[4,6]{1,0:T(4,128)} %add_subtract_fusion) | copy-start | bytes 292
  57.7 71.6 %copy-start.6 = (bf16[512,4,128]{0,2,1:T(8,128)(2,1)}, bf16[512,4,128]{0,2,1:T(8,128)(2,1)S(1)}, u32[]{:S(2)}) copy-start(bf16[512,4,128]{0,2,1:T(8,128)(2,1)S(1)} %add_convert_fusion) | copy-start | bytes 1572868
  70.4 55.8 %collective-permute-start.8 = (bf16[6,2,128,128]{3,0,2,1:T(8,128)(2,1)}, bf16[6,2,128,128]{3,0,2,1:T(8,128)(2,1)S(1)}, u32[]{:S(2)}, u32[]{:S(2)}) collective-permute-start(bf16[6,2,128,128]{3,0,2,1:T(8,128)(2,1)} %get-tuple-element.10), channel_id=1, source_target_pairs={{0,32},{32,64},{64,96},{96,0},{1,33},{33,65},{65,97},{97,1},{2,34}... | collective-permute-start | bytes 1179656 | tf_op jit(solution)/shard_map/ppermute | solution.py:64
  71.6 56.0 %collective-permute-start.10 = (bf16[6,2,128,128]{3,0,2,1:T(8,128)(2,1)}, bf16[6,2,128,128]{3,0,2,1:T(8,128)(2,1)}, u32[]{:S(2)}, u32[]{:S(2)}) collective-permute-start(bf16[6,2,128,128]{3,0,2,1:T(8,128)(2,1)} %get-tuple-element.11), channel_id=1, source_target_pairs={{0,96},{32,0},{64,32},{96,64},{1,97},{33,1},{65,33},{97,65},{2,98}... | collective-permute-start | bytes 1179656 | tf_op jit(solution)/shard_map/ppermute | solution.py:64
  73.0 60.9 %collective-permute-start.9 = (bf16[6,2,128,128]{3,0,2,1:T(8,128)(2,1)}, bf16[6,2,128,128]{3,0,2,1:T(8,128)(2,1)}, u32[]{:S(2)}, u32[]{:S(2)}) collective-permute-start(bf16[6,2,128,128]{3,0,2,1:T(8,128)(2,1)} %get-tuple-element.12), channel_id=1, source_target_pairs={{0,64},{32,96},{64,0},{96,32},{1,65},{33,97},{65,1},{97,33},{2,66}... | collective-permute-start | bytes 1179656 | tf_op jit(solution)/shard_map/ppermute | solution.py:64
  122.4 1.3 copy-start.3
  124.9 14.3 %collective-permute-start.5 = (bf16[6,2,128,128]{3,0,2,1:T(8,128)(2,1)}, bf16[6,2,128,128]{3,0,2,1:T(8,128)(2,1)}, u32[]{:S(2)}, u32[]{:S(2)}) collective-permute-start(bf16[6,2,128,128]{3,0,2,1:T(8,128)(2,1)} %get-tuple-element.7), channel_id=1, source_target_pairs={{0,32},{32,64},{64,96},{96,0},{1,33},{33,65},{65,97},{97,1},{2,34}... | collective-permute-start | bytes 1179656 | tf_op jit(solution)/shard_map/ppermute | solution.py:64
  126.2 13.0 %collective-permute-start.7 = (bf16[6,2,128,128]{3,0,2,1:T(8,128)(2,1)}, bf16[6,2,128,128]{3,0,2,1:T(8,128)(2,1)}, u32[]{:S(2)}, u32[]{:S(2)}) collective-permute-start(bf16[6,2,128,128]{3,0,2,1:T(8,128)(2,1)} %get-tuple-element.8), channel_id=1, source_target_pairs={{0,96},{32,0},{64,32},{96,64},{1,97},{33,1},{65,33},{97,65},{2,98}... | collective-permute-start | bytes 1179656 | tf_op jit(solution)/shard_map/ppermute | solution.py:64
  127.6 24.0 %collective-permute-start.6 = (bf16[6,2,128,128]{3,0,2,1:T(8,128)(2,1)}, bf16[6,2,128,128]{3,0,2,1:T(8,128)(2,1)}, u32[]{:S(2)}, u32[]{:S(2)}) collective-permute-start(bf16[6,2,128,128]{3,0,2,1:T(8,128)(2,1)} %get-tuple-element.9), channel_id=1, source_target_pairs={{0,64},{32,96},{64,0},{96,32},{1,65},{33,97},{65,1},{97,33},{2,66}... | collective-permute-start | bytes 1179656 | tf_op jit(solution)/shard_map/ppermute | solution.py:64
  134.0 19.7 %copy-start.7 = (bf16[512,4,128]{0,2,1:T(8,128)(2,1)S(1)}, bf16[512,4,128]{0,2,1:T(8,128)(2,1)}, u32[]{:S(2)}) copy-start(bf16[512,4,128]{0,2,1:T(8,128)(2,1)} %copy-done.6) | copy-start | bytes 1572868
  153.4 2.3 %copy-start.8 = (bf16[512,4,128]{0,2,1:T(8,128)(2,1)S(1)}, bf16[512,4,128]{0,2,1:T(8,128)(2,1)}, u32[]{:S(2)}) copy-start(bf16[512,4,128]{0,2,1:T(8,128)(2,1)} %copy-done.6) | copy-start | bytes 1572868
  153.4 2.3 %copy-start.9 = (bf16[1,512,512]{1,2,0:T(8,128)(2,1)S(1)}, bf16[1,512,512]{1,2,0:T(8,128)(2,1)}, u32[]{:S(2)}) copy-start(bf16[1,512,512]{1,2,0:T(8,128)(2,1)} %get-tuple-element.14) | copy-start | bytes 1572868
  153.5 2.3 %copy-start.20 = (f32[512,4]{0,1:T(4,128)S(1)}, f32[512,4]{0,1:T(4,128)}, u32[]{:S(2)}) copy-start(f32[512,4]{0,1:T(4,128)} %fusion.90) | copy-start | bytes 24580
  153.5 2.3 %copy-start.21 = (f32[1,4,4,128]{3,1,2,0:T(4,128)S(1)}, f32[1,4,4,128]{3,1,2,0:T(4,128)}, u32[]{:S(2)}) copy-start(f32[1,4,4,128]{3,1,2,0:T(4,128)} %copy.104) | copy-start | bytes 24580
  153.7 2.1 %copy-start.10 = (bf16[1,512,512]{1,2,0:T(8,128)(2,1)S(1)}, bf16[1,512,512]{1,2,0:T(8,128)(2,1)}, u32[]{:S(2)}) copy-start(bf16[1,512,512]{1,2,0:T(8,128)(2,1)} %get-tuple-element.13) | copy-start | bytes 1572868
  155.8 3.1 %copy-start.22 = (f32[512,4]{0,1:T(4,128)S(1)}, f32[512,4]{0,1:T(4,128)}, u32[]{:S(2)}) copy-start(f32[512,4]{0,1:T(4,128)} %fusion.89) | copy-start | bytes 24580
  158.9 2.8 %copy-start.5 = (bf16[512,1024]{1,0:T(8,128)(2,1)S(1)}, bf16[512,1024]{1,0:T(8,128)(2,1)}, u32[]{:S(2)}) copy-start(bf16[512,1024]{1,0:T(8,128)(2,1)} %param.24) | copy-start | bytes 3145732
  161.7 6.1 %copy-start.2 = (bf16[256,1024]{1,0:T(8,128)(2,1)S(1)}, bf16[256,1024]{1,0:T(8,128)(2,1)}, u32[]{:S(2)}) copy-start(bf16[256,1024]{1,0:T(8,128)(2,1)} %param.13) | copy-start | bytes 1572868
  162.5 6.8 %copy-start.24 = (f32[1,1024]{1,0:T(1,128)S(1)}, f32[1,1024]{1,0:T(1,128)}, u32[]{:S(2)}) copy-start(f32[1,1024]{1,0:T(1,128)} %get-tuple-element.19) | copy-start | bytes 12292
  163.6 4.2 %collective-permute-start.11 = (f32[256,1024]{1,0:T(8,128)}, f32[256,1024]{1,0:T(8,128)}, u32[]{:S(2)}, u32[]{:S(2)}) collective-permute-start(f32[256,1024]{1,0:T(8,128)} %constant_dynamic-slice_fusion), channel_id=1, source_target_pairs={{0,1},{1,0},{2,3},{3,2},{4,5},{5,4},{6,7},{7,6},{8,9},{9,8},{10,11... | collective-permute-start | bytes 3145736 | tf_op jit(solution)/shard_map/ppermute | solution.py:21
  181.0 3.9 %copy-start.1 = (bf16[3,1024,512]{2,1,0:T(8,128)(2,1)S(1)}, bf16[3,1024,512]{2,1,0:T(8,128)(2,1)}, u32[]{:S(2)}) copy-start(bf16[3,1024,512]{2,1,0:T(8,128)(2,1)} %param.15) | copy-start | bytes 9437188
Sparse Core Ops, SparseCore 0:
  9.5 54.7 all-gather.4
  66.4 51.1 all-gather.2

commit v4 on v1

--- a/solution.py
+++ b/solution.py
@@ -4,6 +4,8 @@
 import jax.numpy as jnp
 import numpy as np
 from jax import lax
+from jax.experimental import pallas as pl
+from jax.experimental.pallas import tpu as pltpu
 from jax.sharding import Mesh
 from jax.sharding import PartitionSpec as P
 
@@ -25,6 +27,44 @@
     first = jnp.where(col == 0, mine, other)
     second = jnp.where(col == 0, other, mine)
     return jnp.concatenate([first, second], axis=0)
+
+
+def pick_states(index, valid, plane, lines):
+    slots = index.shape[0]
+    per_line = slots // lines
+    block = plane.shape[1:]
+
+    def body(index_ref, valid_ref, plane_ref, *rest):
+        outs = rest[:lines]
+        zero_ref, sems = rest[lines:]
+        zero_ref[...] = jnp.zeros(block, plane.dtype)
+        for s in range(slots):
+            dst = outs[s // per_line].at[s % per_line]
+
+            @pl.when(valid_ref[s] != 0)
+            def _():
+                pltpu.make_async_copy(plane_ref.at[index_ref[s]], dst, sems.at[s]).start()
+
+            @pl.when(valid_ref[s] == 0)
+            def _():
+                pltpu.make_async_copy(zero_ref, dst, sems.at[s]).start()
+
+        for s in range(slots):
+            dst = outs[s // per_line].at[s % per_line]
+            pltpu.make_async_copy(zero_ref, dst, sems.at[s]).wait()
+
+    out_shape = [jax.ShapeDtypeStruct((per_line,) + block, plane.dtype) for _ in range(lines)]
+    return pl.pallas_call(
+        body,
+        out_shape=out_shape,
+        grid_spec=pltpu.PrefetchScalarGridSpec(
+            num_scalar_prefetch=2,
+            grid=(),
+            in_specs=[pl.BlockSpec(memory_space=pl.ANY)],
+            out_specs=[pl.BlockSpec(memory_space=pl.ANY) for _ in range(lines)],
+            scratch_shapes=[pltpu.VMEM(block, plane.dtype), pltpu.SemaphoreType.DMA((slots,))],
+        ),
+    )(index, valid, plane)
 
 
 def on_device(
@@ -57,12 +97,23 @@
 
     plane = lax.all_gather(caches, ("y", "x"), axis=0, tiled=True)
     per_plane = plane.shape[0]
-    line_index = lax.all_gather(request_cache_index[0], "z", axis=0)
-    local = line_index - lax.axis_index("z") * per_plane
-    valid = (local >= 0) & (local < per_plane)
-    picked = plane[jnp.clip(local, 0, per_plane - 1)]
-    slots = jnp.where(valid[:, :, None, None, None], picked, jnp.zeros_like(picked))
-    states = lax.psum_scatter(slots, "z", scatter_dimension=0, tiled=True)[0]
+    z_count = lax.axis_size("z")
+    z_here = lax.axis_index("z")
+    own_index = request_cache_index[0]
+    shifts = range(1, z_count)
+
+    def along_z(value, d):
+        return lax.ppermute(value, "z", perm=[(i, (i + d) % z_count) for i in range(z_count)])
+
+    shifted = {d: along_z(own_index, d) for d in shifts}
+    line_rows = jnp.stack([own_index] + [shifted[z_count - d] for d in shifts])
+    local = line_rows - z_here * per_plane
+    valid = ((local >= 0) & (local < per_plane)).astype(jnp.int32)
+    picked = pick_states(jnp.clip(local, 0, per_plane - 1).reshape(-1), valid.reshape(-1), plane, z_count)
+    states = picked[0].astype(jnp.float32)
+    for d in shifts:
+        states = states + along_z(picked[d], d).astype(jnp.float32)
+    states = states.astype(jnp.bfloat16)
 
     normalized_rows = rms_scale(tokens, norm_gain_pair[0])
     gathered = pair_rows(normalized_rows, swap(normalized_rows), col)
@@ -96,10 +147,8 @@
     up_chosen = jnp.einsum(
         "gq,qjl->gjl", adapter_onehot, adapter_up_factor, preferred_element_type=jnp.float32
     ).astype(jnp.bfloat16)
-    delta_all = jnp.einsum(
-        "tr,src->tsc", low_rank_delta, up_chosen, preferred_element_type=jnp.float32
-    )
-    delta = jnp.sum(member[:, :, None] * delta_all, axis=1)
+    masked_low = low_rank_delta[:, None, :] * member.astype(jnp.bfloat16)[:, :, None]
+    delta = jnp.einsum("tsr,src->tc", masked_low, up_chosen, preferred_element_type=jnp.float32)
     queries = (projected[0] + delta).astype(jnp.bfloat16).reshape(group, local_heads, head_size)
     keys = projected[1].astype(jnp.bfloat16).reshape(group, local_heads, head_size)
     values = projected[2].astype(jnp.bfloat16).reshape(group, local_heads, head_size)
@@ -113,8 +162,11 @@
     start_hot = (positions[None, :] == starts[:, None]).astype(jnp.float32)
     start_level = jnp.sum(start_hot[:, :, None] * before[None, :, :], axis=1)
     level = running - jnp.sum(member[:, :, None] * start_level[None, :, :], axis=1)
-    from_state = jnp.einsum("thi,shij->tshj", queries, states, preferred_element_type=jnp.float32)
-    carried = jnp.sum(member[:, :, None, None] * from_state, axis=1) * jnp.exp(level)[:, :, None]
+    masked_queries = queries[:, None, :, :] * member.astype(jnp.bfloat16)[:, :, None, None]
+    from_state = jnp.einsum(
+        "tshi,shij->thj", masked_queries, states, preferred_element_type=jnp.float32
+    )
+    carried = from_state * jnp.exp(level)[:, :, None]
 
     scores = jnp.einsum("qhd,khd->hqk", queries, keys, preferred_element_type=jnp.float32) * scale
     allowed = (segment[:, None] == segment[None, :]) & (positions[None, :] <= positions[:, None])

time: 178 us -> 183 us (1.028)
  the two profiles are of different devices: /device:TPU:1 before, /device:TPU:21 now
where the time goes in v4:
time: 183 us; the launch traced here: 181 us
  waiting for transfers between devices  46.5 us (25%)
  matrix products  42.2 us (23%)
  Pallas kernels  21.9 us (12%)
  other arithmetic  21.4 us (12%)
  starting transfers between devices  20.8 us (11%)
  local copies, waits for them, and re-layouts  14.6 us (8%)
  between operations  13.7 us (7%)
    ppermute x6, waiting for transfers between devices, along_z(): lax.ppermute(value, 'z', perm=[(i, (i + d) % z_count) for i in range(z_co...  23.7 us
    pallas_call x1, Pallas kernels, pick_states(): pl.pallas_call(body, out_shape=out_shape, grid_spec=pltpu.PrefetchScalarG...  21.9 us
    all_gather x1, waiting for transfers between devices, on_device(): plane = lax.all_gather(caches, ('y', 'x'), axis=0, tiled=True)  19.4 us
    ppermute x6, starting transfers between devices, along_z(): lax.ppermute(value, 'z', perm=[(i, (i + d) % z_count) for i in range(z_co...  17.5 us
    dot_general x2, matrix products, feed_half(): jnp.einsum('td,kdf->ktf', normed_two, weight[:2], preferred_element_type=...  8.73 us
    dot_general x2, matrix products, feed_half(): jnp.einsum('tf,df->td', hidden, weight[2], preferred_element_type=jnp.flo...  6.71 us
    unnamed x48, local copies, waits for them, and re-layouts  6.05 us
    dot_general x1, matrix products, on_device(): jnp.einsum('td,kdc->ktc', gathered, query_key_value_weight, preferred_ele...  4.74 us
  transfers between devices with their start and end apart: 11, of which 5 were waited for; matrix products, arithmetic and copies ran while one was open for 37% of the time, Pallas kernels for 12%

profile of v4, /device:TPU:21, one launch (start us, length us, event | category | flops | bytes accessed | tf_op | source)
XLA Modules:
  0.0 181.0 jit_solution(15650503383055764668)
XLA Ops:
  6.5 0.7 all-gather.2.cloned.1.call-update
  7.3 1.7 collective-permute-start.4
  9.0 3.3 %collective-permute-start.3 = (s32[6]{0:T(128)}, s32[6]{0:T(128)}, u32[]{:S(2)}, u32[]{:S(2)}) collective-permute-start(s32[6]{0:T(128)} %bitcast.154), channel_id=1, source_target_pairs={{0,64},{32,96},{64,0},{96,32},{1,65},{33,97},{65,1},{97,33},{2,66}... | collective-permute-start | bytes 80 | tf_op jit(solution)/shard_map/ppermute | solution.py:106
  12.3 0.7 collective-permute-start.2
  13.0 1.2 fusion.46
  14.2 1.4 fusion.108
  15.6 0.6 copy-done.9
  16.2 2.0 %fusion.48 = bf16[256,1024]{1,0:T(8,128)(2,1)} fusion(bf16[256,1024]{1,0:T(8,128)(2,1)} %param.13, f32[1024]{0:T(1024)S(1)} %bitcast.144, f32[256]{0:T(256)S(1)} %add_rsqrt_fusion.2), kind=kLoop, calls=%fused_computation.57 | loop fusion | flops 1048576 | bytes 1053696 | tf_op jit(solution)/shard_map/convert_element_type | solution.py:19
  18.2 1.5 collective-permute-start
  19.7 2.8 %copy.49 = bf16[32,1024,16]{1,0,2:T(8,128)(2,1)} copy(bf16[32,1024,16]{1,2,0:T(8,128)(2,1)} %param.18) | data formatting | bytes 2097152 | tf_op args[5]
  22.7 0.2 reduce-window.14
  22.9 0.6 iota_add_fusion.1
  23.6 0.7 fusion.73
  24.2 0.7 fusion.72
  24.9 0.2 fusion.56
  25.1 2.5 %convolution_convert_fusion = bf16[6,16,512]{2,0,1:T(8,128)(2,1)S(1)} fusion(bf16[64,16,512]{2,1,0:T(8,128)(2,1)} %param.19, s32[6]{0:T(128)} %bitcast.148), kind=kOutput, calls=%fused_computation.53 | convolution fusion | flops 6340992 | bytes 1146904 | tf_op jit(solution)/shard_map/gq,qjl->gjl/dot_general | solution.py:147
  27.6 0.5 iota_add_fusion
  28.1 3.3 %fusion.86 = f32[6,1024,16]{1,0,2:T(8,128)} fusion(s32[32]{0:T(128)} %iota_add_fusion.1, s32[6]{0:T(128)} %bitcast.149, bf16[32,1024,16]{1,2,0:T(8,128)(2,1)} %param.18), kind=kOutput, calls=%fused_computation.113 | convolution fusion | flops 6291648 | bytes 1441944 | tf_op jit(solution)/shard_map/sa,adr->sdr/dot_general | solution.py:137
  31.4 0.5 collective-permute-start.9
  31.9 1.3 and_convert_fusion
  33.2 1.4 reshape.336.valid_ref
  34.5 1.3 broadcast_clamp_fusion
  35.8 1.3 min.12.index_ref
  37.1 1.5 broadcast_select_fusion.1
  38.7 0.8 copy-done.5
  39.5 1.1 convolution_bitcast_fusion.2
  40.6 0.6 copy-done.10
  41.2 0.7 fusion.104
  41.9 1.3 reshape.333
  43.2 3.1 %reduce-window.18 = f32[4,4,128]{2,1,0:T(4,128)} reduce-window(f32[4,4,128]{2,1,0:T(4,128)} %reshape.333, f32[]{:T(128)} %constant.19.clone.1), window={size=1x1x128 pad=0_0x0_0x127_0}, to_apply=%region_6.7 | reduce-window | flops 260096 | bytes 16388 | tf_op jit(solution)/shard_map/reduce-window.1
  46.3 1.4 slice_reduce_fusion
  47.7 1.4 reduce-window.19
  49.1 0.8 add_bitcast_fusion
  49.9 0.6 copy.78
  50.5 0.8 bitcast_subtract_fusion.1
  51.3 0.8 multiply_reduce_fusion.3
  52.1 1.3 fusion.80
  53.5 0.6 fusion.81
  54.2 4.7 %fusion.109 = (bf16[3,512,512]{1,2,0:T(8,128)(2,1)S(1)}, f32[3,512,512]{1,2,0:T(8,128)}) fusion(bf16[3,1024,512]{2,1,0:T(8,128)(2,1)S(1)} %copy-done, bf16[256,1024]{1,0:T(8,128)(2,1)} %copy-done.7, bf16[256,1024]{1,0:T(8,128)(2,1)} %copy-done.5), kind=kOutput, calls=%fused_computation.144 | convolution fusion | flops 1613496320 | bytes 8912896 | tf_op jit(solution)/shard_map/td,kdc->ktc/dot_general | solution.py:127
  59.0 1.7 fusion.45
  60.8 0.5 fusion.64
  61.3 19.4 %all-gather.2.cloned.1.call-done.plane_ref = bf16[64,4,128,128]{3,2,1,0:T(8,128)(2,1)} async-done(((bf16[4,4,128,128]{3,2,1,0:T(8,128)(2,1)}), bf16[64,4,128,128]{3,2,1,0:T(8,128)(2,1)}) %all-gather.2.cloned.1.call-update) | async-done | bytes 8388624 | tf_op jit(solution)/shard_map/all_gather | solution.py:98
  80.7 21.9 %shard_map.127 = (bf16[6,4,128,128]{3,2,1,0:T(8,128)(2,1)}, bf16[6,4,128,128]{3,2,1,0:T(8,128)(2,1)}, bf16[6,4,128,128]{3,2,1,0:T(8,128)(2,1)}, bf16[6,4,128,128]{3,2,1,0:T(8,128)(2,1)}) custom-call(s32[24]{0:T(128)} %min.12.index_ref, s32[24]{0:T(128)} %reshape.336.valid_ref, bf16[64,4,128,128]{3,2,1,0:T(8,128)(2,1)} %all-gather.2.cloned.1.call-done.plane_ref), custom_call_target="tpu_custom_call" | custom-call | tf_op jit(solution)/shard_map/pallas_call | solution.py:57
  102.6 9.3 %collective-permute-start.5 = (bf16[6,4,128,128]{3,2,1,0:T(8,128)(2,1)}, bf16[6,4,128,128]{3,2,1,0:T(8,128)(2,1)}, u32[]{:S(2)}, u32[]{:S(2)}) collective-permute-start(bf16[6,4,128,128]{3,2,1,0:T(8,128)(2,1)} %get-tuple-element.10), channel_id=1, source_target_pairs={{0,32},{32,64},{64,96},{96,0},{1,33},{33,65},{65,97},{97,1},{2,34}... | collective-permute-start | bytes 2359304 | tf_op jit(solution)/shard_map/ppermute | solution.py:106
  111.9 2.5 %collective-permute-start.7 = (bf16[6,4,128,128]{3,2,1,0:T(8,128)(2,1)}, bf16[6,4,128,128]{3,2,1,0:T(8,128)(2,1)}, u32[]{:S(2)}, u32[]{:S(2)}) collective-permute-start(bf16[6,4,128,128]{3,2,1,0:T(8,128)(2,1)} %get-tuple-element.12), channel_id=1, source_target_pairs={{0,96},{32,0},{64,32},{96,64},{1,97},{33,1},{65,33},{97,65},{2,98}... | collective-permute-start | bytes 2359304 | tf_op jit(solution)/shard_map/ppermute | solution.py:106
  114.4 1.6 fusion.43
  115.9 0.3 copy.58
  116.2 3.6 %fusion.110 = (f32[4,512]{1,0:T(4,128)S(1)}, f32[4,512,512]{1,2,0:T(8,128)}) fusion(pred[512,512]{0,1:T(8,128)(4,1)S(1)} %fusion.56, bf16[512,4,128]{0,2,1:T(8,128)(2,1)S(1)} %bitcast.135, bf16[512,4,128]{0,2,1:T(8,128)(2,1)S(1)} %bitcast.140), kind=kOutput, calls=%fused_computation.145 | convolution fusion | flops 272630272 | bytes 5513216 | tf_op jit(solution)/shard_map/sub | solution.py:175
  119.9 2.9 %fusion.29 = f32[512,4,128]{0,2,1:T(8,128)} fusion(bf16[512,4,128]{0,2,1:T(8,128)(2,1)S(1)} %bitcast.138, f32[4,512]{1,0:T(4,128)S(1)} %bitcast.147, pred[512,512]{0,1:T(8,128)(4,1)S(1)} %fusion.56, bf16[512,4,128]{0,2,1:T(8,128)(2,1)S(1)} %bitcast.136, bf16[512,4,128]{0,2,1:T(8,128)(2,1)S(1)} %bitcast.141), kind=kOutput, calls=%fused_computation.40 | convolution fusion | flops 542113792 | bytes 2891776 | tf_op jit(solution)/shard_map/hqk,khd->qhd/dot_general | solution.py:180
  122.7 16.7 %collective-permute-done.5 = bf16[6,4,128,128]{3,2,1,0:T(8,128)(2,1)} collective-permute-done((bf16[6,4,128,128]{3,2,1,0:T(8,128)(2,1)}, bf16[6,4,128,128]{3,2,1,0:T(8,128)(2,1)}, u32[]{:S(2)}, u32[]{:S(2)}) %collective-permute-start.5) | collective-permute-done | bytes 786464 | tf_op jit(solution)/shard_map/ppermute | solution.py:106
  139.5 5.8 %collective-permute-done.6 = bf16[6,4,128,128]{3,2,1,0:T(8,128)(2,1)} collective-permute-done((bf16[6,4,128,128]{3,2,1,0:T(8,128)(2,1)}, bf16[6,4,128,128]{3,2,1,0:T(8,128)(2,1)}, u32[]{:S(2)}, u32[]{:S(2)}) %collective-permute-start.6) | collective-permute-done | bytes 786464 | tf_op jit(solution)/shard_map/ppermute | solution.py:106
  145.2 1.2 collective-permute-done.7
  146.4 3.6 %multiply_reduce_fusion = (f32[512,4]{0,1:T(4,128)S(1)}, f32[512,4,128]{0,2,1:T(8,128)S(1)}) fusion(f32[512,4,128]{0,2,1:T(8,128)} %fusion.29, f32[512,4]{0,1:T(4,128)S(1)} %copy-done.13, bf16[512,6]{0,1:T(8,128)(2,1)S(1)} %copy-done.11, bf16[512,4,128]{2,0,1:T(8,128)(2,1)S(1)} %copy.58, bf16[6,4,128,128]{3,2,1,0:T(8,128)(2,1)} %collective-permute-done.7, ...), kind=kOutput, calls=%fused_computation.67 | convolution fusion | flops 408418304 | bytes 5789696 | tf_op jit(solution)/shard_map/tshi,shij->thj/dot_general | solution.py:166
  150.1 0.6 fusion.42
  150.8 0.6 copy-done.4
  151.3 0.7 fusion.113
  152.1 1.2 constant_dynamic-slice_fusion
  153.3 1.3 collective-permute-start.8
  154.5 2.6 %collective-permute-done.8 = f32[256,1024]{1,0:T(8,128)} collective-permute-done((f32[256,1024]{1,0:T(8,128)}, f32[256,1024]{1,0:T(8,128)}, u32[]{:S(2)}, u32[]{:S(2)}) %collective-permute-start.8) | collective-permute-done | bytes 1048608 | tf_op jit(solution)/shard_map/ppermute | solution.py:23
  157.1 1.5 fusion.50
  158.7 4.4 %fusion.5 = f32[2,256,1408]{2,1,0:T(8,128)S(1)} fusion(bf16[3,1024,1408]{2,1,0:T(8,128)(2,1)} %param.25, bf16[256,1024]{1,0:T(8,128)(2,1)S(1)} %get-tuple-element.14, f32[1024]{0:T(1024)S(1)} %bitcast.151, f32[256]{0:T(256)S(1)} %add_rsqrt_fusion.1), kind=kOutput, calls=%fused_computation.9 | convolution fusion | flops 1477443584 | bytes 9180160 | tf_op jit(solution)/shard_map/td,kdf->ktf/dot_general | solution.py:194
  163.0 2.9 %fusion.15 = f32[256,1024]{1,0:T(8,128)S(1)} fusion(bf16[3,1024,1408]{2,1,0:T(8,128)(2,1)} %param.25, f32[2,256,1408]{2,1,0:T(8,128)S(1)} %fusion.5), kind=kOutput, calls=%fused_computation.16 | convolution fusion | flops 740360192 | bytes 6815744 | tf_op jit(solution)/shard_map/tf,df->td/dot_general | solution.py:198
  165.9 4.4 %fusion.8 = f32[2,256,1408]{2,1,0:T(8,128)S(1)} fusion(bf16[3,1024,1408]{2,1,0:T(8,128)(2,1)} %collective-permute-done.9, bf16[256,1024]{1,0:T(8,128)(2,1)S(1)} %get-tuple-element.14, f32[1024]{0:T(1024)S(1)} %bitcast.152, f32[256]{0:T(256)S(1)} %add_rsqrt_fusion.1), kind=kOutput, calls=%fused_computation.10 | convolution fusion | flops 1477443584 | bytes 9180160 | tf_op jit(solution)/shard_map/td,kdf->ktf/dot_general | solution.py:194
  170.3 3.8 %fusion.44 = bf16[256,1024]{1,0:T(8,128)(2,1)} fusion(f32[256,1024]{1,0:T(8,128)S(1)} %fusion.15, bf16[3,1024,1408]{2,1,0:T(8,128)(2,1)} %collective-permute-done.9, bf16[256,1024]{1,0:T(8,128)(2,1)S(1)} %get-tuple-element.14, f32[2,256,1408]{2,1,0:T(8,128)S(1)} %fusion.8), kind=kOutput, calls=%fused_computation.50 | convolution fusion | flops 741408768 | bytes 7864320 | tf_op jit(solution)/shard_map/tf,df->td/dot_general | solution.py:198
  (62 shorter events, 0.7 us)
Async XLA Ops:
  6.5 47.6 %copy-start = (bf16[3,1024,512]{2,1,0:T(8,128)(2,1)S(1)}, bf16[3,1024,512]{2,1,0:T(8,128)(2,1)}, u32[]{:S(2)}) copy-start(bf16[3,1024,512]{2,1,0:T(8,128)(2,1)} %param.15) | copy-start | bytes 9437188
  6.5 16.0 %copy-start.21 = (s32[1,2,3]{2,1,0:T(2,128)S(1)}, s32[1,2,3]{2,1,0:T(2,128)}, u32[]{:S(2)}) copy-start(s32[1,2,3]{2,1,0:T(2,128)} %param.20) | copy-start | bytes 76
  6.5 74.2 %all-gather.2.cloned.1.call-start = ((), (), s32[]{:S(2)}) async-start(), calls=%async_computation | async-start | bytes 8912896 | tf_op jit(solution)/shard_map/all_gather | solution.py:98
  7.3 24.1 %collective-permute-start.4 = (s32[6]{0:T(128)}, s32[6]{0:T(128)}, u32[]{:S(2)}, u32[]{:S(2)}) collective-permute-start(s32[6]{0:T(128)} %bitcast.153), channel_id=1, source_target_pairs={{0,32},{32,64},{64,96},{96,0},{1,33},{33,65},{65,97},{97,1},{2,34}... | collective-permute-start | bytes 80 | tf_op jit(solution)/shard_map/ppermute | solution.py:106
  9.0 22.9 %collective-permute-start.3 = (s32[6]{0:T(128)}, s32[6]{0:T(128)}, u32[]{:S(2)}, u32[]{:S(2)}) collective-permute-start(s32[6]{0:T(128)} %bitcast.154), channel_id=1, source_target_pairs={{0,64},{32,96},{64,0},{96,32},{1,65},{33,97},{65,1},{97,33},{2,66}... | collective-permute-start | bytes 80 | tf_op jit(solution)/shard_map/ppermute | solution.py:106
  12.3 19.6 %collective-permute-start.2 = (s32[6]{0:T(128)}, s32[6]{0:T(128)}, u32[]{:S(2)}, u32[]{:S(2)}) collective-permute-start(s32[6]{0:T(128)} %bitcast.155), channel_id=1, source_target_pairs={{0,96},{32,0},{64,32},{96,64},{1,97},{33,1},{65,33},{97,65},{2,98}... | collective-permute-start | bytes 80 | tf_op jit(solution)/shard_map/ppermute | solution.py:106
  14.2 4.0 %copy-start.12 = (f32[256]{0:T(256)}, f32[256]{0:T(256)S(1)}, u32[]{:S(2)}) copy-start(f32[256]{0:T(256)S(1)} %add_rsqrt_fusion.2) | copy-start | bytes 3076
  15.6 0.6 copy-start.9
  18.2 18.9 %collective-permute-start = (bf16[256,1024]{1,0:T(8,128)(2,1)}, bf16[256,1024]{1,0:T(8,128)(2,1)}, u32[]{:S(2)}, u32[]{:S(2)}) collective-permute-start(bf16[256,1024]{1,0:T(8,128)(2,1)} %fusion.48), channel_id=1, source_target_pairs={{0,1},{1,0},{2,3},{3,2},{4,5},{5,4},{6,7},{7,6},{8,9},{9,8},{10,11... | collective-permute-start | bytes 1572872 | tf_op jit(solution)/shard_map/ppermute | solution.py:23
  22.5 36.5 %collective-permute-start.1 = (bf16[32,1024,16]{1,0,2:T(8,128)(2,1)}, bf16[32,1024,16]{1,0,2:T(8,128)(2,1)}, u32[]{:S(2)}, u32[]{:S(2)}) collective-permute-start(bf16[32,1024,16]{1,0,2:T(8,128)(2,1)} %copy.49), channel_id=1, source_target_pairs={{0,1},{1,0},{2,3},{3,2},{4,5},{5,4},{6,7},{7,6},{8,9},{9,8},{10,11... | collective-permute-start | bytes 3145736 | tf_op jit(solution)/shard_map/ppermute | solution.py:23
  31.4 134.5 %collective-permute-start.9 = (bf16[3,1024,1408]{2,1,0:T(8,128)(2,1)}, bf16[3,1024,1408]{2,1,0:T(8,128)(2,1)}, u32[]{:S(2)}, u32[]{:S(2)}) collective-permute-start(bf16[3,1024,1408]{2,1,0:T(8,128)(2,1)} %param.25), channel_id=1, source_target_pairs={{0,1},{1,0},{2,3},{3,2},{4,5},{5,4},{6,7},{7,6},{8,9},{9,8},{10,11... | collective-permute-start | bytes 25952264 | tf_op jit(solution)/shard_map/ppermute | solution.py:23
  37.1 4.1 %copy-start.18 = (f32[4]{0:T(128)S(1)}, f32[4]{0:T(128)}, u32[]{:S(2)}) copy-start(f32[4]{0:T(128)} %param.17) | copy-start | bytes 52
  38.7 0.8 copy-start.5
  38.7 1.9 %copy-start.7 = (bf16[256,1024]{1,0:T(8,128)(2,1)}, bf16[256,1024]{1,0:T(8,128)(2,1)S(1)}, u32[]{:S(2)}) copy-start(bf16[256,1024]{1,0:T(8,128)(2,1)S(1)} %get-tuple-element.18) | copy-start | bytes 1572868
  40.6 0.6 copy-start.10
  54.2 4.8 %copy-start.3 = (f32[6,1024,16]{1,0,2:T(8,128)S(1)}, f32[6,1024,16]{1,0,2:T(8,128)}, u32[]{:S(2)}) copy-start(f32[6,1024,16]{1,0,2:T(8,128)} %fusion.86) | copy-start | bytes 1179652
  54.2 4.8 %copy-start.16 = (s32[1,6]{1,0:T(1,128)S(1)}, s32[1,6]{1,0:T(1,128)}, u32[]{:S(2)}) copy-start(s32[1,6]{1,0:T(1,128)} %param.21) | copy-start | bytes 76
  54.2 4.9 %copy-start.19 = (s32[32]{0:T(128)S(1)}, s32[32]{0:T(128)}, u32[]{:S(2)}) copy-start(s32[32]{0:T(128)} %iota_add_fusion) | copy-start | bytes 388
  58.9 1.9 %copy-start.6 = (bf16[256,1024]{1,0:T(8,128)(2,1)S(1)}, bf16[256,1024]{1,0:T(8,128)(2,1)}, u32[]{:S(2)}) copy-start(bf16[256,1024]{1,0:T(8,128)(2,1)} %copy-done.5) | copy-start | bytes 1572868
  58.9 1.9 %copy-start.8 = (bf16[256,1024]{1,0:T(8,128)(2,1)S(1)}, bf16[256,1024]{1,0:T(8,128)(2,1)}, u32[]{:S(2)}) copy-start(bf16[256,1024]{1,0:T(8,128)(2,1)} %copy-done.7) | copy-start | bytes 1572868
  61.3 53.1 %copy-start.11 = (bf16[512,6]{0,1:T(8,128)(2,1)S(1)}, bf16[512,6]{0,1:T(8,128)(2,1)}, u32[]{:S(2)}) copy-start(bf16[512,6]{0,1:T(8,128)(2,1)} %get-tuple-element.22) | copy-start | bytes 18436
  102.6 36.8 %collective-permute-start.5 = (bf16[6,4,128,128]{3,2,1,0:T(8,128)(2,1)}, bf16[6,4,128,128]{3,2,1,0:T(8,128)(2,1)}, u32[]{:S(2)}, u32[]{:S(2)}) collective-permute-start(bf16[6,4,128,128]{3,2,1,0:T(8,128)(2,1)} %get-tuple-element.10), channel_id=1, source_target_pairs={{0,32},{32,64},{64,96},{96,0},{1,33},{33,65},{65,97},{97,1},{2,34}... | collective-permute-start | bytes 2359304 | tf_op jit(solution)/shard_map/ppermute | solution.py:106
  111.9 33.4 %collective-permute-start.6 = (bf16[6,4,128,128]{3,2,1,0:T(8,128)(2,1)}, bf16[6,4,128,128]{3,2,1,0:T(8,128)(2,1)}, u32[]{:S(2)}, u32[]{:S(2)}) collective-permute-start(bf16[6,4,128,128]{3,2,1,0:T(8,128)(2,1)} %get-tuple-element.11), channel_id=1, source_target_pairs={{0,64},{32,96},{64,0},{96,32},{1,65},{33,97},{65,1},{97,33},{2,66}... | collective-permute-start | bytes 2359304 | tf_op jit(solution)/shard_map/ppermute | solution.py:106
  111.9 34.5 %collective-permute-start.7 = (bf16[6,4,128,128]{3,2,1,0:T(8,128)(2,1)}, bf16[6,4,128,128]{3,2,1,0:T(8,128)(2,1)}, u32[]{:S(2)}, u32[]{:S(2)}) collective-permute-start(bf16[6,4,128,128]{3,2,1,0:T(8,128)(2,1)} %get-tuple-element.12), channel_id=1, source_target_pairs={{0,96},{32,0},{64,32},{96,64},{1,97},{33,1},{65,33},{97,65},{2,98}... | collective-permute-start | bytes 2359304 | tf_op jit(solution)/shard_map/ppermute | solution.py:106
  116.2 3.6 %copy-start.15 = (f32[1,4,4,128]{3,1,2,0:T(4,128)S(1)}, f32[1,4,4,128]{3,1,2,0:T(4,128)}, u32[]{:S(2)}) copy-start(f32[1,4,4,128]{3,1,2,0:T(4,128)} %copy.78) | copy-start | bytes 24580
  119.8 26.6 %copy-start.13 = (f32[512,4]{0,1:T(4,128)S(1)}, f32[512,4]{0,1:T(4,128)}, u32[]{:S(2)}) copy-start(f32[512,4]{0,1:T(4,128)} %fusion.81) | copy-start | bytes 24580
  119.8 26.6 %copy-start.20 = (bf16[6,4,128,128]{3,2,1,0:T(8,128)(2,1)S(1)}, bf16[6,4,128,128]{3,2,1,0:T(8,128)(2,1)}, u32[]{:S(2)}) copy-start(bf16[6,4,128,128]{3,2,1,0:T(8,128)(2,1)} %get-tuple-element.9) | copy-start | bytes 2359300
  146.4 3.7 %copy-start.14 = (f32[512,4]{0,1:T(4,128)S(1)}, f32[512,4]{0,1:T(4,128)}, u32[]{:S(2)}) copy-start(f32[512,4]{0,1:T(4,128)} %fusion.80) | copy-start | bytes 24580
  146.4 3.7 %copy-start.22 = (f32[4,512,512]{1,2,0:T(8,128)S(1)}, f32[4,512,512]{1,2,0:T(8,128)}, u32[]{:S(2)}) copy-start(f32[4,512,512]{1,2,0:T(8,128)} %get-tuple-element.26) | copy-start | bytes 12582916
  150.1 1.2 copy-start.4
  151.3 5.8 %copy-start.2 = (bf16[256,1024]{1,0:T(8,128)(2,1)S(1)}, bf16[256,1024]{1,0:T(8,128)(2,1)}, u32[]{:S(2)}) copy-start(bf16[256,1024]{1,0:T(8,128)(2,1)} %param.13) | copy-start | bytes 1572868
  152.1 6.6 %copy-start.17 = (f32[1,1024]{1,0:T(1,128)S(1)}, f32[1,1024]{1,0:T(1,128)}, u32[]{:S(2)}) copy-start(f32[1,1024]{1,0:T(1,128)} %get-tuple-element.19) | copy-start | bytes 12292
  153.3 3.9 %collective-permute-start.8 = (f32[256,1024]{1,0:T(8,128)}, f32[256,1024]{1,0:T(8,128)}, u32[]{:S(2)}, u32[]{:S(2)}) collective-permute-start(f32[256,1024]{1,0:T(8,128)} %constant_dynamic-slice_fusion), channel_id=1, source_target_pairs={{0,1},{1,0},{2,3},{3,2},{4,5},{5,4},{6,7},{7,6},{8,9},{9,8},{10,11... | collective-permute-start | bytes 3145736 | tf_op jit(solution)/shard_map/ppermute | solution.py:23
  170.3 3.9 %copy-start.1 = (bf16[3,1024,512]{2,1,0:T(8,128)(2,1)S(1)}, bf16[3,1024,512]{2,1,0:T(8,128)(2,1)}, u32[]{:S(2)}) copy-start(bf16[3,1024,512]{2,1,0:T(8,128)(2,1)} %param.15) | copy-start | bytes 9437188
Sparse Core Ops, SparseCore 0:
  9.5 71.1 all-gather.1
